TPU v7x, 256 devices: a whole 4x4x8 slice. The times are simulated.
256 devices in a mesh: gx: 8 (over x, z_hi), gy: 4 (over z_lo), gz: 8 (over y, core).
Axes of the slice: x: 4, y: 4, z: 8 (z_hi: 2, z_lo: 4; z = z_hi * 4 + z_lo), core: 2. Of those that a mesh axis runs over, the one named last changes fastest.
Arguments:
- plus_blocks: float32 [8, 4, 8, 3, 4, 256, 256], P('gx', 'gy', 'gz'), may hold values from -0.1 to 4, as said below
- minus_blocks: float32 [8, 4, 8, 3, 4, 256, 256], P('gx', 'gy', 'gz'), may hold values from -0.1 to 4, as said below
- inner_blocks: float32 [8, 4, 8, 2, 8, 256, 256], P('gx', 'gy', 'gz'), may hold values from -0.1 to 4, as said below
- initial_subspace: float32 [8, 4, 8, 20, 16, 256], P('gx', 'gy', 'gz'), may hold values from -6 to 6
- picks: int32 [8, 4, 8, 20, 8], P('gx', 'gy', 'gz'), may hold values from 0 to 15, all different within a row
- owner: int32 [8, 4, 8, 20], P('gx', 'gy', 'gz'), may hold values from 0 to 127
- material_class: int32 [8, 4, 8], P('gx', 'gy', 'gz'), may hold values from 0 to 3
- coef: float32 [4], replicated, may hold values from 1 to 4
Outputs:
- constraints: float32 [8, 4, 8, 20, 8, 256], P('gx', 'gy', 'gz')
- coarse: float32 [8, 4, 128, 64], P('gx', 'gy', 'gz')
Inputs may be any that keep to these rules, and one draw needn't show every extreme that they name: Each face's picks are distinct. `plus_blocks`: symmetric blocks, diagonal entries from 1 to 4, off-diagonal entries within -0.1 to 0.1. `minus_blocks`: symmetric blocks, diagonal entries from 1 to 4, off-diagonal entries within -0.1 to 0.1. `inner_blocks`: symmetric blocks, diagonal entries from 1 to 4, off-diagonal entries within -0.1 to 0.1.
All inputs are finite; a program needn't handle non-finite values.
Results may differ from a plain program's by a relative error of at most 0.00012.
Values sent between devices are 32-bit elements; how exact they have to be, the bound alone decides.
No kernel may reach another device: no remote copies, remote signals or barrier semaphores. Data moves between devices by JAX's collectives and lax.ppermute only.
A program may use at most 128 MiB of HBM per device.

v0:
```python
import functools
import math

import jax
import jax.numpy as jnp
from jax import lax
from jax.experimental import pallas as pl
from jax.experimental.pallas import tpu as pltpu
from jax.sharding import PartitionSpec as P

ITERS = 4
CROWS = 16
HIGHEST = lax.Precision.HIGHEST


def passed_along(block, axis, distance):
    devices = range(lax.axis_size(axis))
    route = [(i - distance, i) for i in devices if i - distance in devices]
    return lax.ppermute(block, axis, route)


def eliminate(gram):
    faces, count, _ = gram.shape
    sub = lax.broadcasted_iota(jnp.int32, (faces, count, count), 1)
    lane = lax.broadcasted_iota(jnp.int32, (faces, count, count), 2)
    left = gram
    right = (sub == lane).astype(jnp.float32)
    for j in range(count):
        row_l = jnp.sum(jnp.where(sub == j, left, 0.0), axis=1, keepdims=True)
        row_r = jnp.sum(jnp.where(sub == j, right, 0.0), axis=1, keepdims=True)
        pivot = jnp.sum(jnp.where(lane[:, :1] == j, row_l, 0.0), axis=2, keepdims=True)
        inv = 1.0 / jnp.sqrt(pivot)
        col = jnp.sum(jnp.where(lane == j, left, 0.0), axis=2, keepdims=True) * inv
        col = jnp.where(sub[:, :, :1] > j, col, 0.0)
        row_l = row_l * inv
        row_r = row_r * inv
        left = jnp.where(sub == j, row_l, left - col * row_l)
        right = jnp.where(sub == j, row_r, right - col * row_r)
    return right


def face_kernel(scal_ref, picks_ref, a_ref, b_ref, v0_ref, c_ref, e_ref, m_scr, v_scr, w_scr, g_scr):
    faces = a_ref.shape[0]
    nsel = c_ref.shape[1]
    own = scal_ref[0]

    def build(f, carry):
        m_scr[f] = own * a_ref[f] + scal_ref[1 + f] * b_ref[f]
        v_scr[f] = v0_ref[f]
        return carry

    lax.fori_loop(0, faces, build, 0)

    def image(f, carry):
        w = jnp.dot(v_scr[f], m_scr[f], precision=HIGHEST, preferred_element_type=jnp.float32)
        w_scr[f] = w
        g_scr[f] = lax.dot_general(
            w, w, (((1,), (1,)), ((), ())), precision=HIGHEST, preferred_element_type=jnp.float32
        )
        return carry

    def solve(f, carry):
        v_scr[f] = jnp.dot(g_scr[f], w_scr[f], precision=HIGHEST, preferred_element_type=jnp.float32)
        return carry

    for iteration in range(ITERS):
        lax.fori_loop(0, faces, image, 0)
        g_scr[...] = eliminate(g_scr[...])
        lax.fori_loop(0, faces, solve, 0)

    def finish(f, carry):
        rows = [v_scr[f, pl.ds(picks_ref[f * nsel + s], 1), :] for s in range(nsel)]
        picked = jnp.concatenate(rows, axis=0)
        c_ref[f] = picked
        images = jnp.dot(picked, m_scr[f], precision=HIGHEST, preferred_element_type=jnp.float32)
        block = lax.dot_general(
            picked, images, (((1,), (1,)), ((), ())), precision=HIGHEST, preferred_element_type=jnp.float32
        )
        e_ref[f] = block / own
        return carry

    lax.fori_loop(0, faces, finish, 0)


def run_faces(scalars, picks, first, second, start):
    faces, width = first.shape[0], first.shape[-1]
    count = start.shape[1]
    nsel = picks.shape[1]
    vmem = pltpu.MemorySpace.VMEM
    smem = pltpu.MemorySpace.SMEM
    return pl.pallas_call(
        face_kernel,
        out_shape=(
            jax.ShapeDtypeStruct((faces, nsel, width), jnp.float32),
            jax.ShapeDtypeStruct((faces, nsel, nsel), jnp.float32),
        ),
        in_specs=[
            pl.BlockSpec(memory_space=smem),
            pl.BlockSpec(memory_space=smem),
            pl.BlockSpec(memory_space=vmem),
            pl.BlockSpec(memory_space=vmem),
            pl.BlockSpec(memory_space=vmem),
        ],
        out_specs=(pl.BlockSpec(memory_space=vmem), pl.BlockSpec(memory_space=vmem)),
        scratch_shapes=[
            pltpu.VMEM((faces, width, width), jnp.float32),
            pltpu.VMEM((faces, count, width), jnp.float32),
            pltpu.VMEM((faces, count, width), jnp.float32),
            pltpu.VMEM((faces, count, count), jnp.float32),
        ],
        compiler_params=pltpu.CompilerParams(vmem_limit_bytes=60 * 1024 * 1024),
    )(scalars, picks.reshape(-1), first, second, start)


def per_device(
    plus_blocks, minus_blocks, inner_blocks, initial_subspace, picks, owner, material_class, coef
):
    plus_local = plus_blocks[0, 0, 0]
    minus_local = minus_blocks[0, 0, 0]
    inner_local = inner_blocks[0, 0, 0]
    basis_vectors = initial_subspace[0, 0, 0]
    picks_local = picks[0, 0, 0]
    dims, crossing, width = plus_local.shape[0], plus_local.shape[1], plus_local.shape[-1]
    matches = material_class.reshape(()) == jnp.arange(coef.shape[0], dtype=jnp.int32)
    own_scale = jnp.sum(jnp.where(matches, coef, 0.0))
    axes = ("gx", "gy", "gz")
    partners = [passed_along(minus_local[a], axes[a], -1) for a in range(dims)]
    next_scales = [passed_along(own_scale, axes[a], -1) for a in range(dims)]

    n_inner = inner_local.shape[1]
    inner_scal = jnp.full((1 + n_inner,), own_scale, jnp.float32)
    inner_c, inner_e = run_faces(
        inner_scal, picks_local[dims * crossing :], inner_local[0], inner_local[1],
        basis_vectors[dims * crossing :],
    )
    cross_scal = jnp.concatenate(
        [own_scale[None]] + [jnp.broadcast_to(s, (crossing,)) for s in next_scales]
    )
    cross_c, cross_e = run_faces(
        cross_scal, picks_local[: dims * crossing], plus_local.reshape(dims * crossing, width, width),
        jnp.stack(partners).reshape(dims * crossing, width, width), basis_vectors[: dims * crossing],
    )
    picked_modes = jnp.concatenate([cross_c, inner_c], axis=0)
    blocks = jnp.concatenate([cross_e, inner_e], axis=0)
    faces = blocks.shape[0]
    flat = blocks.reshape(faces, -1)
    groups = lax.axis_size("gz")
    rows_all = groups * CROWS
    owner_hot = (owner[0, 0, 0][:, None] == jnp.arange(rows_all, dtype=jnp.int32)).astype(jnp.float32)
    term = jnp.einsum("fr,fe->re", owner_hot, flat, precision=HIGHEST).reshape(groups, CROWS, -1)
    me = lax.axis_index("gz")
    coarse = term[me]
    for shift in range(1, groups):
        part = lax.dynamic_index_in_dim(term, (me + shift) % groups, 0, keepdims=False)
        route = [(i, (i + shift) % groups) for i in range(groups)]
        coarse = coarse + lax.ppermute(part, "gz", route)
    constraints = picked_modes * math.sqrt(width)
    return (constraints[None, None, None], coarse[None, None])


def solution(mesh):
    return jax.shard_map(
        per_device,
        mesh=mesh,
        in_specs=(
            P("gx", "gy", "gz", None, None, None, None),
            P("gx", "gy", "gz", None, None, None, None),
            P("gx", "gy", "gz", None, None, None, None),
            P("gx", "gy", "gz", None, None, None),
            P("gx", "gy", "gz", None, None),
            P("gx", "gy", "gz", None),
            P("gx", "gy", "gz"),
            P(),
        ),
        out_specs=(P("gx", "gy", "gz", None, None, None), P("gx", "gy", "gz", None)),
        check_vma=False,
    )
```

profile of v0, /device:TPU:6, one launch (start us, length us, event | category | flops | bytes accessed | tf_op | source)
XLA Modules:
  0.0 145.8 jit_solution(15705274721054538156)
XLA Ops:
  1.3 1.3 fusion.13
  2.6 0.0 copy-start.2
  2.6 0.0 copy-start
  2.6 9.5 %collective-permute-start = (f32[]{:T(128)}, f32[]{:T(128)}, u32[]{:S(2)}, u32[]{:S(2)}) collective-permute-start(f32[]{:T(128)} %fusion.13), channel_id=1, source_target_pairs={{32,0},{64,32},{96,64},{128,96},{160,128},{192,160},{224,192},{33,... | collective-permute-start | bytes 20 | tf_op jit(solution)/shard_map/ppermute | solution.py:19
  12.1 1.3 collective-permute-start.1
  13.4 3.5 %slice_bitcast_fusion.4 = (f32[4,256,256]{2,1,0:T(8,128)}, f32[4,256,256]{2,1,0:T(8,128)S(1)}, f32[4,256,256]{2,1,0:T(8,128)}) fusion(f32[1,1,1,3,4,256,256]{6,5,4,3,2,1,0:T(8,128)} %param.9), kind=kLoop, calls=%fused_computation.5 | loop fusion | bytes 6291456 | tf_op jit(solution)/shard_map/squeeze | solution.py:127
  16.8 1.9 %collective-permute-start.3 = (f32[4,256,256]{2,1,0:T(8,128)}, f32[4,256,256]{2,1,0:T(8,128)S(1)}, u32[]{:S(2)}, u32[]{:S(2)}) collective-permute-start(f32[4,256,256]{2,1,0:T(8,128)} %get-tuple-element.12), channel_id=1, source_target_pairs={{32,0},{64,32},{96,64},{128,96},{160,128},{192,160},{224,192},{33,... | collective-permute-start | bytes 3145736 | tf_op jit(solution)/shard_map/ppermute | solution.py:19
  18.8 1.3 collective-permute-start.4
  20.1 1.3 collective-permute-start.5
  21.4 0.0 copy-done.2
  21.4 0.1 slice.46
  21.5 0.1 copy.16
  21.6 0.7 reshape.85.picks_ref
  22.3 0.1 copy.17
  22.3 0.6 reshape.87.picks_ref
  23.0 0.0 copy-done
  23.0 0.7 slice_bitcast_fusion.6.v0_ref
  23.6 4.6 %slice_bitcast_fusion = (f32[8,256,256]{2,1,0:T(8,128)}, f32[8,256,256]{2,1,0:T(8,128)}) fusion(f32[1,1,1,2,8,256,256]{6,5,4,3,2,1,0:T(8,128)} %param.10), kind=kLoop, calls=%fused_computation.1 | loop fusion | bytes 8388608 | tf_op jit(solution)/shard_map/squeeze | solution.py:133
  28.2 1.1 broadcast_in_dim.29.scal_ref
  29.3 29.3 %shard_map.96 = (f32[8,8,256]{2,1,0:T(8,128)}, f32[8,8,8]{2,1,0:T(8,128)}) custom-call(f32[9]{0:T(128)} %broadcast_in_dim.29.scal_ref, s32[64]{0:T(128)} %reshape.87.picks_ref, f32[8,256,256]{2,1,0:T(8,128)} %get-tuple-element.11.a_ref, f32[8,256,256]{2,1,0:T(8,128)} %get-tuple-element.10.b_ref, f32[8,16,256]{2,1,0:T(8,128)} %slice_bitcast_fusion.6.v0_ref), custom_call_target="tpu_custom_call" | custom-call | tf_op jit(solution)/shard_map/pallas_call | solution.py:91
  58.7 0.8 copy.19
  59.5 0.7 slice_bitcast_fusion.5.v0_ref
  60.2 0.0 collective-permute-done
  60.2 1.5 %collective-permute-start.2 = (f32[]{:T(128)}, f32[]{:T(128)}, u32[]{:S(2)}, u32[]{:S(2)}) collective-permute-start(f32[]{:T(128)} %fusion.13), channel_id=1, source_target_pairs={{1,0},{2,1},{3,2},{4,3},{5,4},{6,5},{7,6},{9,8},{10,9},{11,10},{12... | collective-permute-start | bytes 20 | tf_op jit(solution)/shard_map/ppermute | solution.py:19
  61.6 0.0 collective-permute-done.1
  61.7 2.3 %collective-permute-done.2 = f32[]{:T(128)} collective-permute-done((f32[]{:T(128)}, f32[]{:T(128)}, u32[]{:S(2)}, u32[]{:S(2)}) %collective-permute-start.2) | collective-permute-done | bytes 36 | tf_op jit(solution)/shard_map/ppermute | solution.py:19
  64.0 0.6 broadcast_in_dim.26
  64.6 0.7 broadcast_in_dim.27
  65.3 0.7 broadcast_in_dim.28
  66.0 1.2 pad_maximum_fusion.1.scal_ref
  67.2 2.8 %collective-permute-done.3 = f32[4,256,256]{2,1,0:T(8,128)S(1)} collective-permute-done((f32[4,256,256]{2,1,0:T(8,128)}, f32[4,256,256]{2,1,0:T(8,128)S(1)}, u32[]{:S(2)}, u32[]{:S(2)}) %collective-permute-start.3) | collective-permute-done | bytes 1048608 | tf_op jit(solution)/shard_map/ppermute | solution.py:19
  69.9 19.2 %collective-permute-done.4 = f32[4,256,256]{2,1,0:T(8,128)S(1)} collective-permute-done((f32[4,256,256]{2,1,0:T(8,128)}, f32[4,256,256]{2,1,0:T(8,128)S(1)}, u32[]{:S(2)}, u32[]{:S(2)}) %collective-permute-start.4) | collective-permute-done | bytes 1048608 | tf_op jit(solution)/shard_map/ppermute | solution.py:19
  89.1 0.0 collective-permute-done.5
  89.1 3.2 %pad_maximum_fusion = f32[3,4,256,256]{3,2,1,0:T(8,128)} fusion(f32[1,4,256,256]{3,2,1,0:T(8,128)} %bitcast.8, f32[1,4,256,256]{3,2,1,0:T(8,128)S(1)} %bitcast.68, f32[1,4,256,256]{3,2,1,0:T(8,128)S(1)} %bitcast.67), kind=kLoop, calls=%fused_computation | loop fusion | flops 1572864 | bytes 6291456 | tf_op jit(solution)/shard_map/stack | solution.py:141
  92.3 0.0 copy-start.3
  92.3 0.0 copy-start.1
  92.3 40.2 %shard_map.95 = (f32[12,8,256]{2,1,0:T(8,128)}, f32[12,8,8]{2,1,0:T(8,128)}) custom-call(f32[13]{0:T(128)} %pad_maximum_fusion.1.scal_ref, s32[96]{0:T(128)} %reshape.85.picks_ref, f32[12,256,256]{2,1,0:T(8,128)} %bitcast.66, f32[12,256,256]{2,1,0:T(8,128)} %bitcast.65, f32[12,16,256]{2,1,0:T(8,128)} %slice_bitcast_fusion.5.v0_ref), custom_call_target="tpu_custom_call" | custom-call | tf_op jit(solution)/shard_map/pallas_call | solution.py:91
  132.5 0.9 copy.18
  133.4 0.0 copy-done.3
  133.4 0.3 fusion
  133.7 1.5 %collective-permute-start.10 = (f32[16,64]{1,0:T(8,128)S(1)}, f32[16,64]{1,0:T(8,128)S(1)}, u32[]{:S(2)}, u32[]{:S(2)}) collective-permute-start(f32[16,64]{1,0:T(8,128)S(1)} %get-tuple-element.18), channel_id=1, source_target_pairs={{0,5},{1,6},{2,7},{3,0},{4,1},{5,2},{6,3},{7,4},{8,13},{9,14},{10,... | collective-permute-start | bytes 12296 | tf_op jit(solution)/shard_map/ppermute | solution.py:156
  135.2 1.7 %collective-permute-start.11 = (f32[16,64]{1,0:T(8,128)S(1)}, f32[16,64]{1,0:T(8,128)S(1)}, u32[]{:S(2)}, u32[]{:S(2)}) collective-permute-start(f32[16,64]{1,0:T(8,128)S(1)} %get-tuple-element.17), channel_id=1, source_target_pairs={{0,6},{1,7},{2,0},{3,1},{4,2},{5,3},{6,4},{7,5},{8,14},{9,15},{10,... | collective-permute-start | bytes 12296 | tf_op jit(solution)/shard_map/ppermute | solution.py:156
  136.9 0.5 collective-permute-start.12
  137.4 0.0 collective-permute-start.6
  137.4 1.6 %collective-permute-start.7 = (f32[16,64]{1,0:T(8,128)S(1)}, f32[16,64]{1,0:T(8,128)S(1)}, u32[]{:S(2)}, u32[]{:S(2)}) collective-permute-start(f32[16,64]{1,0:T(8,128)S(1)} %get-tuple-element.21), channel_id=1, source_target_pairs={{0,2},{1,3},{2,4},{3,5},{4,6},{5,7},{6,0},{7,1},{8,10},{9,11},{10,... | collective-permute-start | bytes 12296 | tf_op jit(solution)/shard_map/ppermute | solution.py:156
  139.0 0.0 collective-permute-done.10
  139.1 1.0 collective-permute-start.8
  140.1 0.0 collective-permute-done.11
  140.1 3.1 %collective-permute-start.9 = (f32[16,64]{1,0:T(8,128)S(1)}, f32[16,64]{1,0:T(8,128)S(1)}, u32[]{:S(2)}, u32[]{:S(2)}) collective-permute-start(f32[16,64]{1,0:T(8,128)S(1)} %get-tuple-element.19), channel_id=1, source_target_pairs={{0,4},{1,5},{2,6},{3,7},{4,0},{5,1},{6,2},{7,3},{8,12},{9,13},{10,... | collective-permute-start | bytes 12296 | tf_op jit(solution)/shard_map/ppermute | solution.py:156
  143.2 0.0 copy-done.1
  143.2 1.6 %maximum_multiply_fusion = f32[1,1,1,20,8,256]{5,4,3,2,1,0:T(8,128)} fusion(f32[1,1,1,8,8,256]{5,4,3,2,1,0:T(8,128)S(1)} %bitcast.70, f32[1,1,1,12,8,256]{5,4,3,2,1,0:T(8,128)} %bitcast.69), kind=kLoop, calls=%fused_computation.7 | loop fusion | flops 81920 | bytes 327680 | tf_op jit(solution)/shard_map/mul | solution.py:157
  144.7 0.0 collective-permute-done.12
  144.7 0.0 collective-permute-done.6
  144.7 0.0 collective-permute-done.7
  144.7 0.0 collective-permute-done.8
  144.8 0.5 collective-permute-done.9
  145.2 0.6 fusion.12
  (2 shorter events, 0.0 us)
Async XLA Ops:
  2.6 18.9 %copy-start.2 = (s32[1,1,1,20,8]{3,4,2,1,0:T(8,128)S(1)}, s32[1,1,1,20,8]{3,4,2,1,0:T(8,128)}, u32[]{:S(2)}) copy-start(s32[1,1,1,20,8]{3,4,2,1,0:T(8,128)} %param.12) | copy-start | bytes 1924
  2.6 20.4 %copy-start = (f32[1,1,1,20,16,256]{5,4,3,2,1,0:T(8,128)S(1)}, f32[1,1,1,20,16,256]{5,4,3,2,1,0:T(8,128)}, u32[]{:S(2)}) copy-start(f32[1,1,1,20,16,256]{5,4,3,2,1,0:T(8,128)} %param.11) | copy-start | bytes 983044
  2.6 57.6 %collective-permute-start = (f32[]{:T(128)}, f32[]{:T(128)}, u32[]{:S(2)}, u32[]{:S(2)}) collective-permute-start(f32[]{:T(128)} %fusion.13), channel_id=1, source_target_pairs={{32,0},{64,32},{96,64},{128,96},{160,128},{192,160},{224,192},{33,... | collective-permute-start | bytes 20 | tf_op jit(solution)/shard_map/ppermute | solution.py:19
  12.1 49.6 %collective-permute-start.1 = (f32[]{:T(128)}, f32[]{:T(128)}, u32[]{:S(2)}, u32[]{:S(2)}) collective-permute-start(f32[]{:T(128)} %fusion.13), channel_id=1, source_target_pairs={{8,0},{16,8},{24,16},{9,1},{17,9},{25,17},{10,2},{18,10},{26,18},{... | collective-permute-start | bytes 20 | tf_op jit(solution)/shard_map/ppermute | solution.py:19
  16.8 53.1 %collective-permute-start.3 = (f32[4,256,256]{2,1,0:T(8,128)}, f32[4,256,256]{2,1,0:T(8,128)S(1)}, u32[]{:S(2)}, u32[]{:S(2)}) collective-permute-start(f32[4,256,256]{2,1,0:T(8,128)} %get-tuple-element.12), channel_id=1, source_target_pairs={{32,0},{64,32},{96,64},{128,96},{160,128},{192,160},{224,192},{33,... | collective-permute-start | bytes 3145736 | tf_op jit(solution)/shard_map/ppermute | solution.py:19
  18.8 70.4 %collective-permute-start.4 = (f32[4,256,256]{2,1,0:T(8,128)}, f32[4,256,256]{2,1,0:T(8,128)S(1)}, u32[]{:S(2)}, u32[]{:S(2)}) collective-permute-start(f32[4,256,256]{2,1,0:T(8,128)} %get-tuple-element.14), channel_id=1, source_target_pairs={{8,0},{16,8},{24,16},{9,1},{17,9},{25,17},{10,2},{18,10},{26,18},{... | collective-permute-start | bytes 3145736 | tf_op jit(solution)/shard_map/ppermute | solution.py:19
  20.1 69.1 %collective-permute-start.5 = (f32[4,256,256]{2,1,0:T(8,128)S(1)}, f32[4,256,256]{2,1,0:T(8,128)}, u32[]{:S(2)}, u32[]{:S(2)}) collective-permute-start(f32[4,256,256]{2,1,0:T(8,128)S(1)} %get-tuple-element.13), channel_id=1, source_target_pairs={{1,0},{2,1},{3,2},{4,3},{5,4},{6,5},{7,6},{9,8},{10,9},{11,10},{12... | collective-permute-start | bytes 3145736 | tf_op jit(solution)/shard_map/ppermute | solution.py:19
  60.2 3.8 %collective-permute-start.2 = (f32[]{:T(128)}, f32[]{:T(128)}, u32[]{:S(2)}, u32[]{:S(2)}) collective-permute-start(f32[]{:T(128)} %fusion.13), channel_id=1, source_target_pairs={{1,0},{2,1},{3,2},{4,3},{5,4},{6,5},{7,6},{9,8},{10,9},{11,10},{12... | collective-permute-start | bytes 20 | tf_op jit(solution)/shard_map/ppermute | solution.py:19
  92.3 41.1 %copy-start.3 = (s32[1,1,1,20]{3,2,1,0:T(1,128)S(1)}, s32[1,1,1,20]{3,2,1,0:T(1,128)}, u32[]{:S(2)}) copy-start(s32[1,1,1,20]{3,2,1,0:T(1,128)} %param.13) | copy-start | bytes 244
  92.3 50.9 %copy-start.1 = (f32[8,8,256]{2,1,0:T(8,128)S(1)}, f32[8,8,256]{2,1,0:T(8,128)}, u32[]{:S(2)}) copy-start(f32[8,8,256]{2,1,0:T(8,128)} %get-tuple-element.7) | copy-start | bytes 196612
  133.7 5.3 %collective-permute-start.10 = (f32[16,64]{1,0:T(8,128)S(1)}, f32[16,64]{1,0:T(8,128)S(1)}, u32[]{:S(2)}, u32[]{:S(2)}) collective-permute-start(f32[16,64]{1,0:T(8,128)S(1)} %get-tuple-element.18), channel_id=1, source_target_pairs={{0,5},{1,6},{2,7},{3,0},{4,1},{5,2},{6,3},{7,4},{8,13},{9,14},{10,... | collective-permute-start | bytes 12296 | tf_op jit(solution)/shard_map/ppermute | solution.py:156
  135.2 4.8 %collective-permute-start.11 = (f32[16,64]{1,0:T(8,128)S(1)}, f32[16,64]{1,0:T(8,128)S(1)}, u32[]{:S(2)}, u32[]{:S(2)}) collective-permute-start(f32[16,64]{1,0:T(8,128)S(1)} %get-tuple-element.17), channel_id=1, source_target_pairs={{0,6},{1,7},{2,0},{3,1},{4,2},{5,3},{6,4},{7,5},{8,14},{9,15},{10,... | collective-permute-start | bytes 12296 | tf_op jit(solution)/shard_map/ppermute | solution.py:156
  136.9 7.8 %collective-permute-start.12 = (f32[16,64]{1,0:T(8,128)S(1)}, f32[16,64]{1,0:T(8,128)S(1)}, u32[]{:S(2)}, u32[]{:S(2)}) collective-permute-start(f32[16,64]{1,0:T(8,128)S(1)} %get-tuple-element.16), channel_id=1, source_target_pairs={{0,7},{1,0},{2,1},{3,2},{4,3},{5,4},{6,5},{7,6},{8,15},{9,8},{10,9... | collective-permute-start | bytes 12296 | tf_op jit(solution)/shard_map/ppermute | solution.py:156
  137.4 7.3 %collective-permute-start.6 = (f32[16,64]{1,0:T(8,128)S(1)}, f32[16,64]{1,0:T(8,128)S(1)}, u32[]{:S(2)}, u32[]{:S(2)}) collective-permute-start(f32[16,64]{1,0:T(8,128)S(1)} %get-tuple-element.15), channel_id=1, source_target_pairs={{0,1},{1,2},{2,3},{3,4},{4,5},{5,6},{6,7},{7,0},{8,9},{9,10},{10,1... | collective-permute-start | bytes 12296 | tf_op jit(solution)/shard_map/ppermute | solution.py:156
  137.4 7.3 %collective-permute-start.7 = (f32[16,64]{1,0:T(8,128)S(1)}, f32[16,64]{1,0:T(8,128)S(1)}, u32[]{:S(2)}, u32[]{:S(2)}) collective-permute-start(f32[16,64]{1,0:T(8,128)S(1)} %get-tuple-element.21), channel_id=1, source_target_pairs={{0,2},{1,3},{2,4},{3,5},{4,6},{5,7},{6,0},{7,1},{8,10},{9,11},{10,... | collective-permute-start | bytes 12296 | tf_op jit(solution)/shard_map/ppermute | solution.py:156
  139.1 5.7 %collective-permute-start.8 = (f32[16,64]{1,0:T(8,128)S(1)}, f32[16,64]{1,0:T(8,128)S(1)}, u32[]{:S(2)}, u32[]{:S(2)}) collective-permute-start(f32[16,64]{1,0:T(8,128)S(1)} %get-tuple-element.20), channel_id=1, source_target_pairs={{0,3},{1,4},{2,5},{3,6},{4,7},{5,0},{6,1},{7,2},{8,11},{9,12},{10,... | collective-permute-start | bytes 12296 | tf_op jit(solution)/shard_map/ppermute | solution.py:156
  140.1 5.2 %collective-permute-start.9 = (f32[16,64]{1,0:T(8,128)S(1)}, f32[16,64]{1,0:T(8,128)S(1)}, u32[]{:S(2)}, u32[]{:S(2)}) collective-permute-start(f32[16,64]{1,0:T(8,128)S(1)} %get-tuple-element.19), channel_id=1, source_target_pairs={{0,4},{1,5},{2,6},{3,7},{4,0},{5,1},{6,2},{7,3},{8,12},{9,13},{10,... | collective-permute-start | bytes 12296 | tf_op jit(solution)/shard_map/ppermute | solution.py:156
where the time goes:
time: 147 us; the launch traced here: 146 us
  Pallas kernels  69.5 us (47%)
  starting transfers between devices  26.2 us (18%)
  waiting for transfers between devices  24.7 us (17%)
  local copies, waits for them, and re-layouts  15.8 us (11%)
  other arithmetic  7.88 us (5%)
  between operations  1.5 us (1%)
    pallas_call x2, Pallas kernels, run_faces(): pl.pallas_call(face_kernel, out_shape=(jax.ShapeDtypeStruct((faces, nsel,...  69.5 us
    ppermute x6, waiting for transfers between devices, passed_along(): return lax.ppermute(block, axis, route)  24.3 us
    ppermute x6, starting transfers between devices, passed_along(): return lax.ppermute(block, axis, route)  16.7 us
    ppermute x7, starting transfers between devices, per_device(): coarse = coarse + lax.ppermute(part, 'gz', route)  9.44 us
    squeeze x1, local copies, waits for them, and re-layouts, per_device(): inner_local[1]  4.57 us
    squeeze x1, local copies, waits for them, and re-layouts, per_device(): partners = [passed_along(minus_local[a], axes[a], -1) for a in range(dims)]  3.48 us
    another operation x1, other arithmetic, per_device(): jnp.stack(partners).reshape(dims * crossing, width, width)  3.19 us
  transfers between devices with their start and end apart: 13, of which 4 were waited for; matrix products, arithmetic and copies ran while one was open for 12% of the time, Pallas kernels for 20%

commit v1 on v0

--- a/solution.py
+++ b/solution.py
@@ -1,4 +1,3 @@
-import functools
 import math
 
 import jax
@@ -39,17 +38,10 @@
     return right
 
 
-def face_kernel(scal_ref, picks_ref, a_ref, b_ref, v0_ref, c_ref, e_ref, m_scr, v_scr, w_scr, g_scr):
-    faces = a_ref.shape[0]
+def iterate(own, picks_ref, pick_base, c_ref, e_ref, m_scr, v_scr, w_scr, g_scr):
+    faces = m_scr.shape[0]
     nsel = c_ref.shape[1]
-    own = scal_ref[0]
-
-    def build(f, carry):
-        m_scr[f] = own * a_ref[f] + scal_ref[1 + f] * b_ref[f]
-        v_scr[f] = v0_ref[f]
-        return carry
-
-    lax.fori_loop(0, faces, build, 0)
+    scale_out = math.sqrt(m_scr.shape[-1])
 
     def image(f, carry):
         w = jnp.dot(v_scr[f], m_scr[f], precision=HIGHEST, preferred_element_type=jnp.float32)
@@ -64,14 +56,14 @@
         return carry
 
     for iteration in range(ITERS):
-        lax.fori_loop(0, faces, image, 0)
+        lax.fori_loop(0, faces, image, 0, unroll=4)
         g_scr[...] = eliminate(g_scr[...])
-        lax.fori_loop(0, faces, solve, 0)
+        lax.fori_loop(0, faces, solve, 0, unroll=4)
 
     def finish(f, carry):
-        rows = [v_scr[f, pl.ds(picks_ref[f * nsel + s], 1), :] for s in range(nsel)]
+        rows = [v_scr[f, pl.ds(picks_ref[pick_base + f * nsel + s], 1), :] for s in range(nsel)]
         picked = jnp.concatenate(rows, axis=0)
-        c_ref[f] = picked
+        c_ref[f] = picked * scale_out
         images = jnp.dot(picked, m_scr[f], precision=HIGHEST, preferred_element_type=jnp.float32)
         block = lax.dot_general(
             picked, images, (((1,), (1,)), ((), ())), precision=HIGHEST, preferred_element_type=jnp.float32
@@ -79,28 +71,61 @@
         e_ref[f] = block / own
         return carry
 
-    lax.fori_loop(0, faces, finish, 0)
-
-
-def run_faces(scalars, picks, first, second, start):
-    faces, width = first.shape[0], first.shape[-1]
-    count = start.shape[1]
-    nsel = picks.shape[1]
+    lax.fori_loop(0, faces, finish, 0, unroll=2)
+
+
+def inner_kernel(scal_ref, picks_ref, inner_ref, v0_ref, c_ref, e_ref, m_scr, v_scr, w_scr, g_scr):
+    faces = m_scr.shape[0]
+    base = v0_ref.shape[0] - faces
+    own = scal_ref[0]
+    for f in range(faces):
+        m_scr[f] = own * inner_ref[0, f] + own * inner_ref[1, f]
+        v_scr[f] = v0_ref[base + f]
+    iterate(own, picks_ref, base * c_ref.shape[1], c_ref, e_ref, m_scr, v_scr, w_scr, g_scr)
+
+
+def unpacked(packed, side, index, pairs):
+    width = packed.shape[-1]
+    row = lax.broadcasted_iota(jnp.int32, (width, width), 0)
+    col = lax.broadcasted_iota(jnp.int32, (width, width), 1)
+    mixed = packed[index % pairs]
+    turned = mixed.T
+    if index < pairs:
+        return jnp.where(col >= row, mixed, turned)
+    diagonal = side[index - pairs : index - pairs + 1, :]
+    return jnp.where(col > row, turned, jnp.where(col == row, diagonal, mixed))
+
+
+def cross_kernel(scal_ref, picks_ref, plus_ref, *refs):
+    dims = plus_ref.shape[0]
+    packed_refs = refs[:dims]
+    side_refs = refs[dims : 2 * dims]
+    v0_ref, c_ref, e_ref, m_scr, v_scr, w_scr, g_scr = refs[2 * dims :]
+    crossing = plus_ref.shape[1]
+    pairs = packed_refs[0].shape[0]
+    own = scal_ref[0]
+    for a in range(dims):
+        side = side_refs[a][...]
+        packed = packed_refs[a]
+        next_scale = side[pairs : pairs + 1, 0:1]
+        for k in range(crossing):
+            f = a * crossing + k
+            m_scr[f] = own * plus_ref[a, k] + next_scale * unpacked(packed, side, k, pairs)
+            v_scr[f] = v0_ref[f]
+    iterate(own, picks_ref, 0, c_ref, e_ref, m_scr, v_scr, w_scr, g_scr)
+
+
+def run_faces(kernel, faces, nsel, width, count, smem_args, vmem_args):
     vmem = pltpu.MemorySpace.VMEM
     smem = pltpu.MemorySpace.SMEM
     return pl.pallas_call(
-        face_kernel,
+        kernel,
         out_shape=(
             jax.ShapeDtypeStruct((faces, nsel, width), jnp.float32),
             jax.ShapeDtypeStruct((faces, nsel, nsel), jnp.float32),
         ),
-        in_specs=[
-            pl.BlockSpec(memory_space=smem),
-            pl.BlockSpec(memory_space=smem),
-            pl.BlockSpec(memory_space=vmem),
-            pl.BlockSpec(memory_space=vmem),
-            pl.BlockSpec(memory_space=vmem),
-        ],
+        in_specs=[pl.BlockSpec(memory_space=smem)] * len(smem_args)
+        + [pl.BlockSpec(memory_space=vmem)] * len(vmem_args),
         out_specs=(pl.BlockSpec(memory_space=vmem), pl.BlockSpec(memory_space=vmem)),
         scratch_shapes=[
             pltpu.VMEM((faces, width, width), jnp.float32),
@@ -109,7 +134,7 @@
             pltpu.VMEM((faces, count, count), jnp.float32),
         ],
         compiler_params=pltpu.CompilerParams(vmem_limit_bytes=60 * 1024 * 1024),
-    )(scalars, picks.reshape(-1), first, second, start)
+    )(*smem_args, *vmem_args)
 
 
 def per_device(
@@ -119,42 +144,48 @@
     minus_local = minus_blocks[0, 0, 0]
     inner_local = inner_blocks[0, 0, 0]
     basis_vectors = initial_subspace[0, 0, 0]
-    picks_local = picks[0, 0, 0]
+    picks_flat = picks[0, 0, 0].reshape(-1)
     dims, crossing, width = plus_local.shape[0], plus_local.shape[1], plus_local.shape[-1]
+    faces_all, count = basis_vectors.shape[0], basis_vectors.shape[1]
+    nsel = picks.shape[-1]
+    pairs = crossing // 2
     matches = material_class.reshape(()) == jnp.arange(coef.shape[0], dtype=jnp.int32)
     own_scale = jnp.sum(jnp.where(matches, coef, 0.0))
+    row = lax.broadcasted_iota(jnp.int32, (width, width), 0)
+    col = lax.broadcasted_iota(jnp.int32, (width, width), 1)
     axes = ("gx", "gy", "gz")
-    partners = [passed_along(minus_local[a], axes[a], -1) for a in range(dims)]
-    next_scales = [passed_along(own_scale, axes[a], -1) for a in range(dims)]
-
+    packed_in = []
+    side_in = []
+    for a in range(dims):
+        halves = minus_local[a]
+        packed = jnp.where(col >= row, halves[:pairs], halves[pairs:])
+        diagonals = jnp.diagonal(halves[pairs:], axis1=1, axis2=2)
+        side = jnp.concatenate([diagonals, jnp.broadcast_to(own_scale, (1, width))], axis=0)
+        packed_in.append(passed_along(packed, axes[a], -1))
+        side_in.append(passed_along(side, axes[a], -1))
+
+    scal = own_scale.reshape(1)
     n_inner = inner_local.shape[1]
-    inner_scal = jnp.full((1 + n_inner,), own_scale, jnp.float32)
     inner_c, inner_e = run_faces(
-        inner_scal, picks_local[dims * crossing :], inner_local[0], inner_local[1],
-        basis_vectors[dims * crossing :],
-    )
-    cross_scal = jnp.concatenate(
-        [own_scale[None]] + [jnp.broadcast_to(s, (crossing,)) for s in next_scales]
+        inner_kernel, n_inner, nsel, width, count, (scal, picks_flat), (inner_local, basis_vectors)
     )
     cross_c, cross_e = run_faces(
-        cross_scal, picks_local[: dims * crossing], plus_local.reshape(dims * crossing, width, width),
-        jnp.stack(partners).reshape(dims * crossing, width, width), basis_vectors[: dims * crossing],
+        cross_kernel, dims * crossing, nsel, width, count, (scal, picks_flat),
+        (plus_local, *packed_in, *side_in, basis_vectors),
     )
-    picked_modes = jnp.concatenate([cross_c, inner_c], axis=0)
+    constraints = jnp.concatenate([cross_c, inner_c], axis=0)
     blocks = jnp.concatenate([cross_e, inner_e], axis=0)
-    faces = blocks.shape[0]
-    flat = blocks.reshape(faces, -1)
+    flat = blocks.reshape(faces_all, -1)
     groups = lax.axis_size("gz")
     rows_all = groups * CROWS
     owner_hot = (owner[0, 0, 0][:, None] == jnp.arange(rows_all, dtype=jnp.int32)).astype(jnp.float32)
     term = jnp.einsum("fr,fe->re", owner_hot, flat, precision=HIGHEST).reshape(groups, CROWS, -1)
     me = lax.axis_index("gz")
-    coarse = term[me]
+    coarse = lax.dynamic_index_in_dim(term, me, 0, keepdims=False)
     for shift in range(1, groups):
         part = lax.dynamic_index_in_dim(term, (me + shift) % groups, 0, keepdims=False)
         route = [(i, (i + shift) % groups) for i in range(groups)]
         coarse = coarse + lax.ppermute(part, "gz", route)
-    constraints = picked_modes * math.sqrt(width)
     return (constraints[None, None, None], coarse[None, None])
 
 

time: 147 us -> 169 us (1.15)
  local copies, waits for them, and re-layouts: 15.8 us -> 63.2 us
  waiting for transfers between devices: 24.7 us -> 0.74 us
  Pallas kernels: 69.5 us -> 66.6 us
  other arithmetic: 7.88 us -> 5.89 us
  starting transfers between devices: 26.2 us -> 27.9 us
    slice x5 -> x4, local copies, waits for them, and re-layouts: 1.57 us -> 50.8 us  [per_device(): packed = jnp.where(col >= row, halves[:pairs], halves[pairs:])]
    ppermute x6, waiting for transfers between devices: 24.3 us -> 0.02 us  [passed_along(): return lax.ppermute(block, axis, route)]
    squeeze x2 -> x0, local copies, waits for them, and re-layouts: 8.05 us -> none  [the longest x1 4.57 us: per_device(): inner_local[1]]
    gather x0 -> x6, local copies, waits for them, and re-layouts: none -> 7.21 us  [per_device(): diagonals = jnp.diagonal(halves[pairs:], axis1=1, axis2=2)]
    another operation x1 -> x0, other arithmetic: 3.19 us -> none  [per_device(): jnp.stack(partners).reshape(dims * crossing, width, width)]
    broadcast_in_dim x4 -> x0, local copies, waits for them, and re-layouts: 3.08 us -> none  [the longest x3 1.94 us: per_device(): jnp.broadcast_to(s, (crossing,))]
    select_n x0 -> x1, other arithmetic: none -> 3.04 us  [per_device(): packed = jnp.where(col >= row, halves[:pairs], halves[pairs:])]
    pallas_call x2, Pallas kernels: 69.5 us -> 66.6 us  [run_faces(): pl.pallas_call(kernel, out_shape=(jax.ShapeDtypeStruct((faces, nsel, widt...]
  transfers between devices with their start and end apart: 13 -> 13, of which waited for: 4 -> 1; matrix products, arithmetic and copies ran while one was open for 12% -> 38% of each run, Pallas kernels for 20% -> 17%
where the time goes in v1:
time: 169 us; the launch traced here: 166 us
  Pallas kernels  66.6 us (39%)
  local copies, waits for them, and re-layouts  63.2 us (37%)
  starting transfers between devices  27.9 us (17%)
  other arithmetic  5.89 us (3%)
    pallas_call x2, Pallas kernels, run_faces(): pl.pallas_call(kernel, out_shape=(jax.ShapeDtypeStruct((faces, nsel, widt...  66.6 us
    slice x4, local copies, waits for them, and re-layouts, per_device(): packed = jnp.where(col >= row, halves[:pairs], halves[pairs:])  50.8 us
    ppermute x6, starting transfers between devices, passed_along(): return lax.ppermute(block, axis, route)  16.6 us
    ppermute x7, starting transfers between devices, per_device(): coarse = coarse + lax.ppermute(part, 'gz', route)  11.3 us
    gather x6, local copies, waits for them, and re-layouts, per_device(): diagonals = jnp.diagonal(halves[pairs:], axis1=1, axis2=2)  7.21 us
  transfers between devices with their start and end apart: 13, of which 1 were waited for; matrix products, arithmetic and copies ran while one was open for 38% of the time, Pallas kernels for 17%

profile of v1, /device:TPU:6, one launch (start us, length us, event | category | flops | bytes accessed | tf_op | source)
XLA Modules:
  0.0 166.3 jit_solution(14391662518937943336)
XLA Ops:
  0.6 0.0 copy-start.7
  0.7 3.0 %bitcast_select_fusion = (f32[2,256,256]{2,1,0:T(8,128)S(1)}, f32[2,256,256]{2,1,0:T(8,128)}, f32[2,256,256]{2,1,0:T(8,128)}) fusion(f32[1,1,1,3,4,256,256]{6,5,4,3,2,1,0:T(8,128)} %param.9, pred[256,256]{1,0:T(8,128)(4,1)S(1)} %iota_compare_fusion), kind=kLoop, calls=%fused_computation.3 | loop fusion | flops 393216 | bytes 4784128 | tf_op jit(solution)/shard_map/jit(_where)/select_n | solution.py:161
  3.7 9.3 %collective-permute-start = (f32[2,256,256]{2,1,0:T(8,128)}, f32[2,256,256]{2,1,0:T(8,128)S(1)}, u32[]{:S(2)}, u32[]{:S(2)}) collective-permute-start(f32[2,256,256]{2,1,0:T(8,128)} %get-tuple-element.12), channel_id=1, source_target_pairs={{32,0},{64,32},{96,64},{128,96},{160,128},{192,160},{224,192},{33,... | collective-permute-start | bytes 1572872 | tf_op jit(solution)/shard_map/ppermute | solution.py:18
  13.1 1.3 collective-permute-start.1
  14.4 1.3 collective-permute-start.2
  15.7 1.5 slice_bitcast_fusion
  17.1 16.4 %copy.26 = f32[2,256,256]{0,2,1:T(8,128)} copy(f32[2,256,256]{2,1,0:T(8,128)S(1)} %get-tuple-element.15) | data formatting | bytes 1048576 | tf_op jit(solution)/shard_map/slice | solution.py:161
  33.6 2.3 %gather_fusion = f32[256,2]{1,0:T(8,128)S(1)} fusion(f32[2,256,256]{0,2,1:T(8,128)} %copy.26, s32[256]{0:T(256)S(1)} %bitcast.68), kind=kCustom, calls=%fused_computation | custom fusion | bytes 6144 | tf_op jit(solution)/shard_map/jit(diagonal)/gather | solution.py:162
  35.9 0.1 copy.27
  36.7 0.0 copy-done.7
  36.7 0.6 fusion.13
  37.3 0.6 concatenate.22
  37.8 1.9 %collective-permute-start.3 = (f32[3,256]{1,0:T(4,128)S(1)}, f32[3,256]{1,0:T(4,128)S(1)}, u32[]{:S(2)}, u32[]{:S(2)}) collective-permute-start(f32[3,256]{1,0:T(4,128)S(1)} %concatenate.22), channel_id=1, source_target_pairs={{32,0},{64,32},{96,64},{128,96},{160,128},{192,160},{224,192},{33,... | collective-permute-start | bytes 9224 | tf_op jit(solution)/shard_map/ppermute | solution.py:18
  39.8 0.0 copy-start.5
  39.8 0.0 copy-start.6
  39.8 16.4 %copy.28 = f32[2,256,256]{0,2,1:T(8,128)} copy(f32[2,256,256]{2,1,0:T(8,128)S(1)} %get-tuple-element.14) | data formatting | bytes 1048576 | tf_op jit(solution)/shard_map/slice | solution.py:161
  56.2 2.3 %gather_fusion.1 = f32[256,2]{1,0:T(8,128)S(1)} fusion(f32[2,256,256]{0,2,1:T(8,128)} %copy.28, s32[256]{0:T(256)S(1)} %bitcast.69), kind=kCustom, calls=%fused_computation.1 | custom fusion | bytes 6144 | tf_op jit(solution)/shard_map/jit(diagonal)/gather | solution.py:162
  58.6 0.1 copy.29
  58.6 0.6 concatenate.23
  59.2 1.3 collective-permute-start.4
  60.6 16.4 %copy.30 = f32[2,256,256]{0,2,1:T(8,128)} copy(f32[2,256,256]{2,1,0:T(8,128)S(1)} %get-tuple-element.13) | data formatting | bytes 1048576 | tf_op jit(solution)/shard_map/slice | solution.py:161
  77.0 2.3 %gather_fusion.2 = f32[256,2]{1,0:T(8,128)S(1)} fusion(f32[2,256,256]{0,2,1:T(8,128)} %copy.30, s32[256]{0:T(256)S(1)} %bitcast.70), kind=kCustom, calls=%fused_computation.2 | custom fusion | bytes 6144 | tf_op jit(solution)/shard_map/jit(diagonal)/gather | solution.py:162
  79.4 0.1 copy.31
  79.4 0.6 concatenate.24
  80.0 0.0 collective-permute-done.3.refs_3_
  80.0 0.0 copy-start.2
  80.0 1.5 collective-permute-start.5
  81.6 0.0 copy-done.5
  81.6 0.1 copy.25
  81.7 0.7 reshape_squeeze.3.picks_ref
  82.3 28.3 %shard_map.96 = (f32[8,8,256]{2,1,0:T(8,128)}, f32[8,8,8]{2,1,0:T(8,128)}) custom-call(f32[1]{0:T(128)} %bitcast.1.scal_ref, s32[160]{0:T(256)} %reshape_squeeze.3.picks_ref, f32[2,8,256,256]{3,2,1,0:T(8,128)} %bitcast.71, f32[20,16,256]{2,1,0:T(8,128)} %bitcast.73), custom_call_target="tpu_custom_call" | custom-call | tf_op jit(solution)/shard_map/pallas_call | solution.py:121
  110.6 0.8 copy.33
  111.4 0.0 collective-permute-done.4.refs_4_
  111.5 0.0 copy-start.3
  111.5 0.0 collective-permute-done.5.refs_5_
  111.5 0.0 copy-start.4
  111.5 0.0 collective-permute-done.refs_0_
  111.5 0.0 copy-start
  111.5 0.0 collective-permute-done.1.refs_1_
  111.5 0.0 collective-permute-done.2.refs_2_
  111.5 0.0 copy-done.2
  111.5 0.5 copy-done.3
  112.0 0.0 copy-done.4
  112.1 0.2 copy-done
  112.3 0.2 copy-done.1
  112.5 38.3 %shard_map.95 = (f32[12,8,256]{2,1,0:T(8,128)}, f32[12,8,8]{2,1,0:T(8,128)}) custom-call(f32[1]{0:T(128)} %bitcast.1.scal_ref, s32[160]{0:T(256)} %reshape_squeeze.3.picks_ref, f32[3,4,256,256]{3,2,1,0:T(8,128)} %bitcast.72, f32[2,256,256]{2,1,0:T(8,128)} %copy-done, f32[2,256,256]{2,1,0:T(8,128)} %copy-done.1, ...), custom_call_target="tpu_custom_call" | custom-call | tf_op jit(solution)/shard_map/pallas_call | solution.py:121
  150.8 0.9 copy.32
  151.7 0.3 fusion
  152.0 4.6 %collective-permute-start.10 = (f32[16,64]{1,0:T(8,128)S(1)}, f32[16,64]{1,0:T(8,128)S(1)}, u32[]{:S(2)}, u32[]{:S(2)}) collective-permute-start(f32[16,64]{1,0:T(8,128)S(1)} %get-tuple-element.19), channel_id=1, source_target_pairs={{0,5},{1,6},{2,7},{3,0},{4,1},{5,2},{6,3},{7,4},{8,13},{9,14},{10,... | collective-permute-start | bytes 12296 | tf_op jit(solution)/shard_map/ppermute | solution.py:188
  156.7 1.1 collective-permute-start.11
  157.7 0.0 collective-permute-start.12
  157.7 0.5 collective-permute-start.6
  158.2 1.0 collective-permute-start.7
  159.2 0.0 collective-permute-done.10
  159.2 1.3 collective-permute-start.8
  160.5 0.0 collective-permute-done.11
  160.5 2.8 %collective-permute-start.9 = (f32[16,64]{1,0:T(8,128)S(1)}, f32[16,64]{1,0:T(8,128)S(1)}, u32[]{:S(2)}, u32[]{:S(2)}) collective-permute-start(f32[16,64]{1,0:T(8,128)S(1)} %get-tuple-element.20), channel_id=1, source_target_pairs={{0,4},{1,5},{2,6},{3,7},{4,0},{5,1},{6,2},{7,3},{8,12},{9,13},{10,... | collective-permute-start | bytes 12296 | tf_op jit(solution)/shard_map/ppermute | solution.py:188
  163.3 1.6 maximum_bitcast_fusion
  164.9 0.0 collective-permute-done.12
  164.9 0.0 collective-permute-done.6
  164.9 0.0 collective-permute-done.7
  164.9 0.0 collective-permute-done.8
  164.9 0.7 collective-permute-done.9
  165.6 0.6 fusion.12
  (6 shorter events, 0.1 us)
Async XLA Ops:
  0.6 36.0 %copy-start.7 = (f32[4]{0:T(128)S(1)}, f32[4]{0:T(128)}, u32[]{:S(2)}) copy-start(f32[4]{0:T(128)} %param.15) | copy-start | bytes 52
  3.7 107.8 %collective-permute-start = (f32[2,256,256]{2,1,0:T(8,128)}, f32[2,256,256]{2,1,0:T(8,128)S(1)}, u32[]{:S(2)}, u32[]{:S(2)}) collective-permute-start(f32[2,256,256]{2,1,0:T(8,128)} %get-tuple-element.12), channel_id=1, source_target_pairs={{32,0},{64,32},{96,64},{128,96},{160,128},{192,160},{224,192},{33,... | collective-permute-start | bytes 1572872 | tf_op jit(solution)/shard_map/ppermute | solution.py:18
  13.1 98.4 %collective-permute-start.1 = (f32[2,256,256]{2,1,0:T(8,128)}, f32[2,256,256]{2,1,0:T(8,128)S(1)}, u32[]{:S(2)}, u32[]{:S(2)}) collective-permute-start(f32[2,256,256]{2,1,0:T(8,128)} %get-tuple-element.11), channel_id=1, source_target_pairs={{8,0},{16,8},{24,16},{9,1},{17,9},{25,17},{10,2},{18,10},{26,18},{... | collective-permute-start | bytes 1572872 | tf_op jit(solution)/shard_map/ppermute | solution.py:18
  14.4 97.2 %collective-permute-start.2 = (f32[2,256,256]{2,1,0:T(8,128)S(1)}, f32[2,256,256]{2,1,0:T(8,128)}, u32[]{:S(2)}, u32[]{:S(2)}) collective-permute-start(f32[2,256,256]{2,1,0:T(8,128)S(1)} %get-tuple-element.10), channel_id=1, source_target_pairs={{1,0},{2,1},{3,2},{4,3},{5,4},{6,5},{7,6},{9,8},{10,9},{11,10},{12... | collective-permute-start | bytes 1572872 | tf_op jit(solution)/shard_map/ppermute | solution.py:18
  37.8 42.2 %collective-permute-start.3 = (f32[3,256]{1,0:T(4,128)S(1)}, f32[3,256]{1,0:T(4,128)S(1)}, u32[]{:S(2)}, u32[]{:S(2)}) collective-permute-start(f32[3,256]{1,0:T(4,128)S(1)} %concatenate.22), channel_id=1, source_target_pairs={{32,0},{64,32},{96,64},{128,96},{160,128},{192,160},{224,192},{33,... | collective-permute-start | bytes 9224 | tf_op jit(solution)/shard_map/ppermute | solution.py:18
  39.8 41.8 %copy-start.5 = (s32[1,1,1,20,8]{3,4,2,1,0:T(8,128)S(1)}, s32[1,1,1,20,8]{3,4,2,1,0:T(8,128)}, u32[]{:S(2)}) copy-start(s32[1,1,1,20,8]{3,4,2,1,0:T(8,128)} %param.12) | copy-start | bytes 1924
  39.8 112.0 %copy-start.6 = (s32[1,1,1,20]{3,2,1,0:T(1,128)S(1)}, s32[1,1,1,20]{3,2,1,0:T(1,128)}, u32[]{:S(2)}) copy-start(s32[1,1,1,20]{3,2,1,0:T(1,128)} %param.13) | copy-start | bytes 244
  59.2 52.2 %collective-permute-start.4 = (f32[3,256]{1,0:T(4,128)S(1)}, f32[3,256]{1,0:T(4,128)S(1)}, u32[]{:S(2)}, u32[]{:S(2)}) collective-permute-start(f32[3,256]{1,0:T(4,128)S(1)} %concatenate.23), channel_id=1, source_target_pairs={{8,0},{16,8},{24,16},{9,1},{17,9},{25,17},{10,2},{18,10},{26,18},{... | collective-permute-start | bytes 9224 | tf_op jit(solution)/shard_map/ppermute | solution.py:18
  80.0 31.5 %copy-start.2 = (f32[3,256]{1,0:T(4,128)}, f32[3,256]{1,0:T(4,128)S(1)}, u32[]{:S(2)}) copy-start(f32[3,256]{1,0:T(4,128)S(1)} %collective-permute-done.3.refs_3_) | copy-start | bytes 9220
  80.0 31.4 %collective-permute-start.5 = (f32[3,256]{1,0:T(4,128)S(1)}, f32[3,256]{1,0:T(4,128)S(1)}, u32[]{:S(2)}, u32[]{:S(2)}) collective-permute-start(f32[3,256]{1,0:T(4,128)S(1)} %concatenate.24), channel_id=1, source_target_pairs={{1,0},{2,1},{3,2},{4,3},{5,4},{6,5},{7,6},{9,8},{10,9},{11,10},{12... | collective-permute-start | bytes 9224 | tf_op jit(solution)/shard_map/ppermute | solution.py:18
  111.5 0.6 copy-start.3
  111.5 0.6 copy-start.4
  111.5 0.8 copy-start
  111.5 1.0 copy-start.1
  152.0 7.2 %collective-permute-start.10 = (f32[16,64]{1,0:T(8,128)S(1)}, f32[16,64]{1,0:T(8,128)S(1)}, u32[]{:S(2)}, u32[]{:S(2)}) collective-permute-start(f32[16,64]{1,0:T(8,128)S(1)} %get-tuple-element.19), channel_id=1, source_target_pairs={{0,5},{1,6},{2,7},{3,0},{4,1},{5,2},{6,3},{7,4},{8,13},{9,14},{10,... | collective-permute-start | bytes 12296 | tf_op jit(solution)/shard_map/ppermute | solution.py:188
  156.7 3.8 %collective-permute-start.11 = (f32[16,64]{1,0:T(8,128)S(1)}, f32[16,64]{1,0:T(8,128)S(1)}, u32[]{:S(2)}, u32[]{:S(2)}) collective-permute-start(f32[16,64]{1,0:T(8,128)S(1)} %get-tuple-element.18), channel_id=1, source_target_pairs={{0,6},{1,7},{2,0},{3,1},{4,2},{5,3},{6,4},{7,5},{8,14},{9,15},{10,... | collective-permute-start | bytes 12296 | tf_op jit(solution)/shard_map/ppermute | solution.py:188
  157.7 7.2 %collective-permute-start.12 = (f32[16,64]{1,0:T(8,128)S(1)}, f32[16,64]{1,0:T(8,128)S(1)}, u32[]{:S(2)}, u32[]{:S(2)}) collective-permute-start(f32[16,64]{1,0:T(8,128)S(1)} %get-tuple-element.17), channel_id=1, source_target_pairs={{0,7},{1,0},{2,1},{3,2},{4,3},{5,4},{6,5},{7,6},{8,15},{9,8},{10,9... | collective-permute-start | bytes 12296 | tf_op jit(solution)/shard_map/ppermute | solution.py:188
  157.7 7.2 %collective-permute-start.6 = (f32[16,64]{1,0:T(8,128)S(1)}, f32[16,64]{1,0:T(8,128)S(1)}, u32[]{:S(2)}, u32[]{:S(2)}) collective-permute-start(f32[16,64]{1,0:T(8,128)S(1)} %get-tuple-element.16), channel_id=1, source_target_pairs={{0,1},{1,2},{2,3},{3,4},{4,5},{5,6},{6,7},{7,0},{8,9},{9,10},{10,1... | collective-permute-start | bytes 12296 | tf_op jit(solution)/shard_map/ppermute | solution.py:188
  158.2 6.7 %collective-permute-start.7 = (f32[16,64]{1,0:T(8,128)S(1)}, f32[16,64]{1,0:T(8,128)S(1)}, u32[]{:S(2)}, u32[]{:S(2)}) collective-permute-start(f32[16,64]{1,0:T(8,128)S(1)} %get-tuple-element.22), channel_id=1, source_target_pairs={{0,2},{1,3},{2,4},{3,5},{4,6},{5,7},{6,0},{7,1},{8,10},{9,11},{10,... | collective-permute-start | bytes 12296 | tf_op jit(solution)/shard_map/ppermute | solution.py:188
  159.2 5.7 %collective-permute-start.8 = (f32[16,64]{1,0:T(8,128)S(1)}, f32[16,64]{1,0:T(8,128)S(1)}, u32[]{:S(2)}, u32[]{:S(2)}) collective-permute-start(f32[16,64]{1,0:T(8,128)S(1)} %get-tuple-element.21), channel_id=1, source_target_pairs={{0,3},{1,4},{2,5},{3,6},{4,7},{5,0},{6,1},{7,2},{8,11},{9,12},{10,... | collective-permute-start | bytes 12296 | tf_op jit(solution)/shard_map/ppermute | solution.py:188
  160.5 5.2 %collective-permute-start.9 = (f32[16,64]{1,0:T(8,128)S(1)}, f32[16,64]{1,0:T(8,128)S(1)}, u32[]{:S(2)}, u32[]{:S(2)}) collective-permute-start(f32[16,64]{1,0:T(8,128)S(1)} %get-tuple-element.20), channel_id=1, source_target_pairs={{0,4},{1,5},{2,6},{3,7},{4,0},{5,1},{6,2},{7,3},{8,12},{9,13},{10,... | collective-permute-start | bytes 12296 | tf_op jit(solution)/shard_map/ppermute | solution.py:188

commit v2 on v1

--- a/solution.py
+++ b/solution.py
@@ -159,7 +159,7 @@
     for a in range(dims):
         halves = minus_local[a]
         packed = jnp.where(col >= row, halves[:pairs], halves[pairs:])
-        diagonals = jnp.diagonal(halves[pairs:], axis1=1, axis2=2)
+        diagonals = jnp.sum(jnp.where(col == row, halves[pairs:], 0.0), axis=1)
         side = jnp.concatenate([diagonals, jnp.broadcast_to(own_scale, (1, width))], axis=0)
         packed_in.append(passed_along(packed, axes[a], -1))
         side_in.append(passed_along(side, axes[a], -1))

time: 169 us -> 132 us (0.78)
  the two profiles are of different devices: /device:TPU:6 before, /device:TPU:160 now
where the time goes in v2:
time: 132 us; the launch traced here: 131 us
  Pallas kernels  66.5 us (50%)
  waiting for transfers between devices  31.4 us (24%)
  starting transfers between devices  21.2 us (16%)
  local copies, waits for them, and re-layouts  5.34 us (4%)
  other arithmetic  4.91 us (4%)
  between operations  1.62 us (1%)
    pallas_call x2, Pallas kernels, run_faces(): pl.pallas_call(kernel, out_shape=(jax.ShapeDtypeStruct((faces, nsel, widt...  66.5 us
    ppermute x6, waiting for transfers between devices, passed_along(): return lax.ppermute(block, axis, route)  29.6 us
    ppermute x6, starting transfers between devices, passed_along(): return lax.ppermute(block, axis, route)  11.7 us
    ppermute x7, starting transfers between devices, per_device(): coarse = coarse + lax.ppermute(part, 'gz', route)  9.47 us
  transfers between devices with their start and end apart: 13, of which 3 were waited for; matrix products, arithmetic and copies ran while one was open for 4% of the time, Pallas kernels for 22%

profile of v2, /device:TPU:160, one launch (start us, length us, event | category | flops | bytes accessed | tf_op | source)
XLA Modules:
  0.0 131.3 jit_solution(5221377855749808789)
XLA Ops:
  0.6 0.0 copy-start.9
  0.6 0.0 copy-start.7
  0.7 2.1 %fusion = (f32[2,256]{1,0:T(2,128)S(1)}, f32[2,256]{1,0:T(2,128)S(1)}, f32[2,256]{1,0:T(2,128)S(1)}, f32[2,256,256]{2,1,0:T(8,128)S(1)}, f32[2,256,256]{2,1,0:T(8,128)S(1)}, /*index=5*/f32[2,256,256]{2,1,0:T(8,128)S(1)}) fusion(f32[1,1,1,3,4,256,256]{6,5,4,3,2,1,0:T(8,128)} %param.9, pred[256,256]{1,0:T(8,128)(4,1)S(1)} %get-tuple-element.26, ...), kind=kLoop, calls=%fused_computation.2 | loop fusion | flops 1178112 | bytes 4855808 | tf_op jit(solution)/shard_map/reduce_sum | solution.py:162
  2.8 1.9 %collective-permute-start = (f32[2,256,256]{2,1,0:T(8,128)S(1)}, f32[2,256,256]{2,1,0:T(8,128)S(1)}, u32[]{:S(2)}, u32[]{:S(2)}) collective-permute-start(f32[2,256,256]{2,1,0:T(8,128)S(1)} %get-tuple-element.16), channel_id=1, source_target_pairs={{32,0},{64,32},{96,64},{128,96},{160,128},{192,160},{224,192},{33,... | collective-permute-start | bytes 1572872 | tf_op jit(solution)/shard_map/ppermute | solution.py:18
  4.8 3.4 %collective-permute-start.1 = (f32[2,256,256]{2,1,0:T(8,128)S(1)}, f32[2,256,256]{2,1,0:T(8,128)S(1)}, u32[]{:S(2)}, u32[]{:S(2)}) collective-permute-start(f32[2,256,256]{2,1,0:T(8,128)S(1)} %get-tuple-element.17), channel_id=1, source_target_pairs={{8,0},{16,8},{24,16},{9,1},{17,9},{25,17},{10,2},{18,10},{26,18},{... | collective-permute-start | bytes 1572872 | tf_op jit(solution)/shard_map/ppermute | solution.py:18
  8.1 1.3 collective-permute-start.2
  10.1 0.0 copy-done.9
  10.1 0.6 fusion.16
  10.7 0.5 concatenate.15
  11.2 1.9 %collective-permute-start.3 = (f32[3,256]{1,0:T(4,128)S(1)}, f32[3,256]{1,0:T(4,128)S(1)}, u32[]{:S(2)}, u32[]{:S(2)}) collective-permute-start(f32[3,256]{1,0:T(4,128)S(1)} %concatenate.15), channel_id=1, source_target_pairs={{32,0},{64,32},{96,64},{128,96},{160,128},{192,160},{224,192},{33,... | collective-permute-start | bytes 9224 | tf_op jit(solution)/shard_map/ppermute | solution.py:18
  13.2 0.5 concatenate.16
  13.7 1.9 %collective-permute-start.4 = (f32[3,256]{1,0:T(4,128)S(1)}, f32[3,256]{1,0:T(4,128)S(1)}, u32[]{:S(2)}, u32[]{:S(2)}) collective-permute-start(f32[3,256]{1,0:T(4,128)S(1)} %concatenate.16), channel_id=1, source_target_pairs={{8,0},{16,8},{24,16},{9,1},{17,9},{25,17},{10,2},{18,10},{26,18},{... | collective-permute-start | bytes 9224 | tf_op jit(solution)/shard_map/ppermute | solution.py:18
  15.7 0.5 concatenate.17
  16.3 29.6 %collective-permute-done.3.refs_3_ = f32[3,256]{1,0:T(4,128)S(1)} collective-permute-done((f32[3,256]{1,0:T(4,128)S(1)}, f32[3,256]{1,0:T(4,128)S(1)}, u32[]{:S(2)}, u32[]{:S(2)}) %collective-permute-start.3) | collective-permute-done | bytes 3104 | tf_op jit(solution)/shard_map/ppermute | solution.py:18
  45.9 0.0 copy-start.4
  45.9 1.3 collective-permute-start.5
  47.2 0.0 copy-done.7
  47.2 0.1 copy.13
  47.3 0.7 reshape_squeeze.3.picks_ref
  48.0 28.3 %shard_map.96 = (f32[8,8,256]{2,1,0:T(8,128)}, f32[8,8,8]{2,1,0:T(8,128)}) custom-call(f32[1]{0:T(128)} %bitcast.1.scal_ref, s32[160]{0:T(256)} %reshape_squeeze.3.picks_ref, f32[2,8,256,256]{3,2,1,0:T(8,128)} %bitcast.67, f32[20,16,256]{2,1,0:T(8,128)} %bitcast.69), custom_call_target="tpu_custom_call" | custom-call | tf_op jit(solution)/shard_map/pallas_call | solution.py:121
  76.2 0.0 copy-start.8
  76.2 0.0 copy-start.3
  76.2 0.9 copy.15
  77.1 0.0 collective-permute-done.4.refs_4_
  77.1 0.0 copy-start.5
  77.1 0.0 collective-permute-done.5.refs_5_
  77.1 0.0 copy-start.6
  77.1 0.0 collective-permute-done.refs_0_
  77.1 0.0 copy-start
  77.2 0.0 collective-permute-done.1.refs_1_
  77.2 0.0 copy-start.1
  77.2 0.0 collective-permute-done.2.refs_2_
  77.2 0.0 copy-start.2
  77.2 0.0 copy-done.4
  77.2 0.5 copy-done.5
  77.7 0.0 copy-done.6
  77.7 0.2 copy-done
  77.9 0.2 copy-done.1
  78.1 0.2 copy-done.2
  78.3 38.3 %shard_map.95 = (f32[12,8,256]{2,1,0:T(8,128)}, f32[12,8,8]{2,1,0:T(8,128)}) custom-call(f32[1]{0:T(128)} %bitcast.1.scal_ref, s32[160]{0:T(256)} %reshape_squeeze.3.picks_ref, f32[3,4,256,256]{3,2,1,0:T(8,128)} %bitcast.68, f32[2,256,256]{2,1,0:T(8,128)} %copy-done, f32[2,256,256]{2,1,0:T(8,128)} %copy-done.1, f32[2,256,256]{2,1,0:T(8,128)} %copy-done.2, ...), custom_call_target="tpu_custom_call" | custom-call | tf_op jit(solution)/shard_map/pallas_call | solution.py:121
  116.6 0.9 copy.14
  117.5 0.0 copy-done.8
  117.5 0.3 fusion.3
  117.8 4.0 %collective-permute-start.10 = (f32[16,64]{1,0:T(8,128)S(1)}, f32[16,64]{1,0:T(8,128)S(1)}, u32[]{:S(2)}, u32[]{:S(2)}) collective-permute-start(f32[16,64]{1,0:T(8,128)S(1)} %get-tuple-element.22), channel_id=1, source_target_pairs={{0,5},{1,6},{2,7},{3,0},{4,1},{5,2},{6,3},{7,4},{8,13},{9,14},{10,... | collective-permute-start | bytes 12296 | tf_op jit(solution)/shard_map/ppermute | solution.py:188
  121.8 1.0 collective-permute-start.11
  122.9 0.0 collective-permute-start.12
  122.9 0.5 collective-permute-start.6
  123.4 1.0 collective-permute-start.7
  124.4 0.0 collective-permute-done.10
  124.4 0.4 collective-permute-start.8
  124.8 0.7 collective-permute-done.11
  125.5 2.5 %collective-permute-start.9 = (f32[16,64]{1,0:T(8,128)S(1)}, f32[16,64]{1,0:T(8,128)S(1)}, u32[]{:S(2)}, u32[]{:S(2)}) collective-permute-start(f32[16,64]{1,0:T(8,128)S(1)} %get-tuple-element.23), channel_id=1, source_target_pairs={{0,4},{1,5},{2,6},{3,7},{4,0},{5,1},{6,2},{7,3},{8,12},{9,13},{10,... | collective-permute-start | bytes 12296 | tf_op jit(solution)/shard_map/ppermute | solution.py:188
  128.0 0.0 copy-done.3
  128.0 1.6 %maximum_bitcast_fusion = f32[1,1,1,20,8,256]{5,4,3,2,1,0:T(8,128)} fusion(f32[8,8,256]{2,1,0:T(8,128)S(1)} %copy-done.3, f32[12,8,256]{2,1,0:T(8,128)} %get-tuple-element.6), kind=kLoop, calls=%fused_computation.11 | loop fusion | flops 40960 | bytes 327680 | tf_op jit(solution)/shard_map/broadcast_in_dim | solution.py:189
  129.6 0.0 collective-permute-done.12
  129.6 0.0 collective-permute-done.6
  129.6 0.0 collective-permute-done.7
  129.6 0.0 collective-permute-done.8
  129.6 1.0 collective-permute-done.9
  130.6 0.6 fusion.15
  (3 shorter events, 0.1 us)
Async XLA Ops:
  0.6 9.5 %copy-start.9 = (f32[4]{0:T(128)S(1)}, f32[4]{0:T(128)}, u32[]{:S(2)}) copy-start(f32[4]{0:T(128)} %param.15) | copy-start | bytes 52
  0.6 46.6 %copy-start.7 = (s32[1,1,1,20,8]{3,4,2,1,0:T(8,128)S(1)}, s32[1,1,1,20,8]{3,4,2,1,0:T(8,128)}, u32[]{:S(2)}) copy-start(s32[1,1,1,20,8]{3,4,2,1,0:T(8,128)} %param.12) | copy-start | bytes 1924
  2.8 74.3 %collective-permute-start = (f32[2,256,256]{2,1,0:T(8,128)S(1)}, f32[2,256,256]{2,1,0:T(8,128)S(1)}, u32[]{:S(2)}, u32[]{:S(2)}) collective-permute-start(f32[2,256,256]{2,1,0:T(8,128)S(1)} %get-tuple-element.16), channel_id=1, source_target_pairs={{32,0},{64,32},{96,64},{128,96},{160,128},{192,160},{224,192},{33,... | collective-permute-start | bytes 1572872 | tf_op jit(solution)/shard_map/ppermute | solution.py:18
  4.8 72.4 %collective-permute-start.1 = (f32[2,256,256]{2,1,0:T(8,128)S(1)}, f32[2,256,256]{2,1,0:T(8,128)S(1)}, u32[]{:S(2)}, u32[]{:S(2)}) collective-permute-start(f32[2,256,256]{2,1,0:T(8,128)S(1)} %get-tuple-element.17), channel_id=1, source_target_pairs={{8,0},{16,8},{24,16},{9,1},{17,9},{25,17},{10,2},{18,10},{26,18},{... | collective-permute-start | bytes 1572872 | tf_op jit(solution)/shard_map/ppermute | solution.py:18
  8.1 69.0 %collective-permute-start.2 = (f32[2,256,256]{2,1,0:T(8,128)S(1)}, f32[2,256,256]{2,1,0:T(8,128)S(1)}, u32[]{:S(2)}, u32[]{:S(2)}) collective-permute-start(f32[2,256,256]{2,1,0:T(8,128)S(1)} %get-tuple-element.18), channel_id=1, source_target_pairs={{1,0},{2,1},{3,2},{4,3},{5,4},{6,5},{7,6},{9,8},{10,9},{11,10},{12... | collective-permute-start | bytes 1572872 | tf_op jit(solution)/shard_map/ppermute | solution.py:18
  11.2 34.7 %collective-permute-start.3 = (f32[3,256]{1,0:T(4,128)S(1)}, f32[3,256]{1,0:T(4,128)S(1)}, u32[]{:S(2)}, u32[]{:S(2)}) collective-permute-start(f32[3,256]{1,0:T(4,128)S(1)} %concatenate.15), channel_id=1, source_target_pairs={{32,0},{64,32},{96,64},{128,96},{160,128},{192,160},{224,192},{33,... | collective-permute-start | bytes 9224 | tf_op jit(solution)/shard_map/ppermute | solution.py:18
  13.7 63.4 %collective-permute-start.4 = (f32[3,256]{1,0:T(4,128)S(1)}, f32[3,256]{1,0:T(4,128)S(1)}, u32[]{:S(2)}, u32[]{:S(2)}) collective-permute-start(f32[3,256]{1,0:T(4,128)S(1)} %concatenate.16), channel_id=1, source_target_pairs={{8,0},{16,8},{24,16},{9,1},{17,9},{25,17},{10,2},{18,10},{26,18},{... | collective-permute-start | bytes 9224 | tf_op jit(solution)/shard_map/ppermute | solution.py:18
  45.9 31.3 %copy-start.4 = (f32[3,256]{1,0:T(4,128)}, f32[3,256]{1,0:T(4,128)S(1)}, u32[]{:S(2)}) copy-start(f32[3,256]{1,0:T(4,128)S(1)} %collective-permute-done.3.refs_3_) | copy-start | bytes 9220
  45.9 31.2 %collective-permute-start.5 = (f32[3,256]{1,0:T(4,128)S(1)}, f32[3,256]{1,0:T(4,128)S(1)}, u32[]{:S(2)}, u32[]{:S(2)}) collective-permute-start(f32[3,256]{1,0:T(4,128)S(1)} %concatenate.17), channel_id=1, source_target_pairs={{1,0},{2,1},{3,2},{4,3},{5,4},{6,5},{7,6},{9,8},{10,9},{11,10},{12... | collective-permute-start | bytes 9224 | tf_op jit(solution)/shard_map/ppermute | solution.py:18
  76.2 41.3 %copy-start.8 = (s32[1,1,1,20]{3,2,1,0:T(1,128)S(1)}, s32[1,1,1,20]{3,2,1,0:T(1,128)}, u32[]{:S(2)}) copy-start(s32[1,1,1,20]{3,2,1,0:T(1,128)} %param.13) | copy-start | bytes 244
  76.2 51.8 %copy-start.3 = (f32[8,8,256]{2,1,0:T(8,128)S(1)}, f32[8,8,256]{2,1,0:T(8,128)}, u32[]{:S(2)}) copy-start(f32[8,8,256]{2,1,0:T(8,128)} %get-tuple-element.7) | copy-start | bytes 196612
  77.1 0.6 copy-start.5
  77.1 0.6 copy-start.6
  77.1 0.8 copy-start
  77.2 1.0 copy-start.1
  77.2 1.1 copy-start.2
  117.8 6.6 %collective-permute-start.10 = (f32[16,64]{1,0:T(8,128)S(1)}, f32[16,64]{1,0:T(8,128)S(1)}, u32[]{:S(2)}, u32[]{:S(2)}) collective-permute-start(f32[16,64]{1,0:T(8,128)S(1)} %get-tuple-element.22), channel_id=1, source_target_pairs={{0,5},{1,6},{2,7},{3,0},{4,1},{5,2},{6,3},{7,4},{8,13},{9,14},{10,... | collective-permute-start | bytes 12296 | tf_op jit(solution)/shard_map/ppermute | solution.py:188
  121.8 3.7 %collective-permute-start.11 = (f32[16,64]{1,0:T(8,128)S(1)}, f32[16,64]{1,0:T(8,128)S(1)}, u32[]{:S(2)}, u32[]{:S(2)}) collective-permute-start(f32[16,64]{1,0:T(8,128)S(1)} %get-tuple-element.21), channel_id=1, source_target_pairs={{0,6},{1,7},{2,0},{3,1},{4,2},{5,3},{6,4},{7,5},{8,14},{9,15},{10,... | collective-permute-start | bytes 12296 | tf_op jit(solution)/shard_map/ppermute | solution.py:188
  122.9 6.7 %collective-permute-start.12 = (f32[16,64]{1,0:T(8,128)S(1)}, f32[16,64]{1,0:T(8,128)S(1)}, u32[]{:S(2)}, u32[]{:S(2)}) collective-permute-start(f32[16,64]{1,0:T(8,128)S(1)} %get-tuple-element.20), channel_id=1, source_target_pairs={{0,7},{1,0},{2,1},{3,2},{4,3},{5,4},{6,5},{7,6},{8,15},{9,8},{10,9... | collective-permute-start | bytes 12296 | tf_op jit(solution)/shard_map/ppermute | solution.py:188
  122.9 6.7 %collective-permute-start.6 = (f32[16,64]{1,0:T(8,128)S(1)}, f32[16,64]{1,0:T(8,128)S(1)}, u32[]{:S(2)}, u32[]{:S(2)}) collective-permute-start(f32[16,64]{1,0:T(8,128)S(1)} %get-tuple-element.19), channel_id=1, source_target_pairs={{0,1},{1,2},{2,3},{3,4},{4,5},{5,6},{6,7},{7,0},{8,9},{9,10},{10,1... | collective-permute-start | bytes 12296 | tf_op jit(solution)/shard_map/ppermute | solution.py:188
  123.4 6.2 %collective-permute-start.7 = (f32[16,64]{1,0:T(8,128)S(1)}, f32[16,64]{1,0:T(8,128)S(1)}, u32[]{:S(2)}, u32[]{:S(2)}) collective-permute-start(f32[16,64]{1,0:T(8,128)S(1)} %get-tuple-element.25), channel_id=1, source_target_pairs={{0,2},{1,3},{2,4},{3,5},{4,6},{5,7},{6,0},{7,1},{8,10},{9,11},{10,... | collective-permute-start | bytes 12296 | tf_op jit(solution)/shard_map/ppermute | solution.py:188
  124.4 5.2 %collective-permute-start.8 = (f32[16,64]{1,0:T(8,128)S(1)}, f32[16,64]{1,0:T(8,128)S(1)}, u32[]{:S(2)}, u32[]{:S(2)}) collective-permute-start(f32[16,64]{1,0:T(8,128)S(1)} %get-tuple-element.24), channel_id=1, source_target_pairs={{0,3},{1,4},{2,5},{3,6},{4,7},{5,0},{6,1},{7,2},{8,11},{9,12},{10,... | collective-permute-start | bytes 12296 | tf_op jit(solution)/shard_map/ppermute | solution.py:188
  125.5 5.2 %collective-permute-start.9 = (f32[16,64]{1,0:T(8,128)S(1)}, f32[16,64]{1,0:T(8,128)S(1)}, u32[]{:S(2)}, u32[]{:S(2)}) collective-permute-start(f32[16,64]{1,0:T(8,128)S(1)} %get-tuple-element.23), channel_id=1, source_target_pairs={{0,4},{1,5},{2,6},{3,7},{4,0},{5,1},{6,2},{7,3},{8,12},{9,13},{10,... | collective-permute-start | bytes 12296 | tf_op jit(solution)/shard_map/ppermute | solution.py:188

commit v3 on v2

--- a/solution.py
+++ b/solution.py
@@ -18,47 +18,61 @@
     return lax.ppermute(block, axis, route)
 
 
-def eliminate(gram):
-    faces, count, _ = gram.shape
-    sub = lax.broadcasted_iota(jnp.int32, (faces, count, count), 1)
-    lane = lax.broadcasted_iota(jnp.int32, (faces, count, count), 2)
-    left = gram
-    right = (sub == lane).astype(jnp.float32)
+GROUP = 8
+
+
+def eliminate(grams, count):
+    state = []
+    for gram in grams:
+        faces = gram.shape[0] // count
+        shape = (faces, count, gram.shape[1])
+        face = lax.broadcasted_iota(jnp.int32, shape, 0)
+        sub = lax.broadcasted_iota(jnp.int32, shape, 1)
+        lane = lax.broadcasted_iota(jnp.int32, shape, 2)
+        base = face * count
+        left = jnp.where(lane // count == face, gram.reshape(shape), 0.0)
+        right = (lane == base + sub).astype(jnp.float32)
+        state.append([left, right, sub, lane, base])
     for j in range(count):
-        row_l = jnp.sum(jnp.where(sub == j, left, 0.0), axis=1, keepdims=True)
-        row_r = jnp.sum(jnp.where(sub == j, right, 0.0), axis=1, keepdims=True)
-        pivot = jnp.sum(jnp.where(lane[:, :1] == j, row_l, 0.0), axis=2, keepdims=True)
-        inv = 1.0 / jnp.sqrt(pivot)
-        col = jnp.sum(jnp.where(lane == j, left, 0.0), axis=2, keepdims=True) * inv
-        col = jnp.where(sub[:, :, :1] > j, col, 0.0)
-        row_l = row_l * inv
-        row_r = row_r * inv
-        left = jnp.where(sub == j, row_l, left - col * row_l)
-        right = jnp.where(sub == j, row_r, right - col * row_r)
-    return right
-
-
-def iterate(own, picks_ref, pick_base, c_ref, e_ref, m_scr, v_scr, w_scr, g_scr):
-    faces = m_scr.shape[0]
+        for item in state:
+            left, right, sub, lane, base = item
+            row_l = jnp.sum(jnp.where(sub == j, left, 0.0), axis=1, keepdims=True)
+            row_r = jnp.sum(jnp.where(sub == j, right, 0.0), axis=1, keepdims=True)
+            at_pivot = lane == base + j
+            pivot = jnp.sum(jnp.where(at_pivot[:, :1], row_l, 0.0), axis=2, keepdims=True)
+            inv = 1.0 / jnp.sqrt(pivot)
+            col = jnp.sum(jnp.where(at_pivot, left, 0.0), axis=2, keepdims=True) * inv
+            col = jnp.where(sub[:, :, :1] > j, col, 0.0)
+            row_l = row_l * inv
+            row_r = row_r * inv
+            item[0] = jnp.where(sub == j, row_l, left - col * row_l)
+            item[1] = jnp.where(sub == j, row_r, right - col * row_r)
+    return [item[1].reshape(item[1].shape[0] * count, -1) for item in state]
+
+
+def iterate(own, picks_ref, pick_base, c_ref, e_ref, m_scr, v_scr, w_scr):
+    faces, count = v_scr.shape[0], v_scr.shape[1]
     nsel = c_ref.shape[1]
     scale_out = math.sqrt(m_scr.shape[-1])
+    spans = [(g, min(g + GROUP, faces)) for g in range(0, faces, GROUP)]
 
     def image(f, carry):
-        w = jnp.dot(v_scr[f], m_scr[f], precision=HIGHEST, preferred_element_type=jnp.float32)
-        w_scr[f] = w
-        g_scr[f] = lax.dot_general(
-            w, w, (((1,), (1,)), ((), ())), precision=HIGHEST, preferred_element_type=jnp.float32
-        )
-        return carry
-
-    def solve(f, carry):
-        v_scr[f] = jnp.dot(g_scr[f], w_scr[f], precision=HIGHEST, preferred_element_type=jnp.float32)
+        w_scr[f] = jnp.dot(v_scr[f], m_scr[f], precision=HIGHEST, preferred_element_type=jnp.float32)
         return carry
 
     for iteration in range(ITERS):
         lax.fori_loop(0, faces, image, 0, unroll=4)
-        g_scr[...] = eliminate(g_scr[...])
-        lax.fori_loop(0, faces, solve, 0, unroll=4)
+        images = [w_scr[g0:g1].reshape((g1 - g0) * count, -1) for g0, g1 in spans]
+        grams = [
+            lax.dot_general(
+                w, w, (((1,), (1,)), ((), ())), precision=HIGHEST, preferred_element_type=jnp.float32
+            )
+            for w in images
+        ]
+        inverses = eliminate(grams, count)
+        for (g0, g1), inverse, w in zip(spans, inverses, images):
+            solved = jnp.dot(inverse, w, precision=HIGHEST, preferred_element_type=jnp.float32)
+            v_scr[g0:g1] = solved.reshape(g1 - g0, count, -1)
 
     def finish(f, carry):
         rows = [v_scr[f, pl.ds(picks_ref[pick_base + f * nsel + s], 1), :] for s in range(nsel)]
@@ -74,21 +88,22 @@
     lax.fori_loop(0, faces, finish, 0, unroll=2)
 
 
-def inner_kernel(scal_ref, picks_ref, inner_ref, v0_ref, c_ref, e_ref, m_scr, v_scr, w_scr, g_scr):
+def inner_kernel(scal_ref, picks_ref, inner_ref, v0_ref, c_ref, e_ref, m_scr, v_scr, w_scr):
     faces = m_scr.shape[0]
     base = v0_ref.shape[0] - faces
     own = scal_ref[0]
     for f in range(faces):
         m_scr[f] = own * inner_ref[0, f] + own * inner_ref[1, f]
         v_scr[f] = v0_ref[base + f]
-    iterate(own, picks_ref, base * c_ref.shape[1], c_ref, e_ref, m_scr, v_scr, w_scr, g_scr)
+    iterate(own, picks_ref, base * c_ref.shape[1], c_ref, e_ref, m_scr, v_scr, w_scr)
 
 
 def unpacked(packed, side, index, pairs):
     width = packed.shape[-1]
     row = lax.broadcasted_iota(jnp.int32, (width, width), 0)
     col = lax.broadcasted_iota(jnp.int32, (width, width), 1)
-    mixed = packed[index % pairs]
+    start = (index % pairs) * width
+    mixed = packed[start : start + width, :]
     turned = mixed.T
     if index < pairs:
         return jnp.where(col >= row, mixed, turned)
@@ -99,20 +114,19 @@
 def cross_kernel(scal_ref, picks_ref, plus_ref, *refs):
     dims = plus_ref.shape[0]
     packed_refs = refs[:dims]
-    side_refs = refs[dims : 2 * dims]
-    v0_ref, c_ref, e_ref, m_scr, v_scr, w_scr, g_scr = refs[2 * dims :]
-    crossing = plus_ref.shape[1]
-    pairs = packed_refs[0].shape[0]
+    v0_ref, c_ref, e_ref, m_scr, v_scr, w_scr = refs[dims:]
+    crossing, width = plus_ref.shape[1], plus_ref.shape[-1]
+    pairs = crossing // 2
     own = scal_ref[0]
     for a in range(dims):
-        side = side_refs[a][...]
         packed = packed_refs[a]
+        side = packed[pairs * width :, :]
         next_scale = side[pairs : pairs + 1, 0:1]
         for k in range(crossing):
             f = a * crossing + k
             m_scr[f] = own * plus_ref[a, k] + next_scale * unpacked(packed, side, k, pairs)
             v_scr[f] = v0_ref[f]
-    iterate(own, picks_ref, 0, c_ref, e_ref, m_scr, v_scr, w_scr, g_scr)
+    iterate(own, picks_ref, 0, c_ref, e_ref, m_scr, v_scr, w_scr)
 
 
 def run_faces(kernel, faces, nsel, width, count, smem_args, vmem_args):
@@ -131,7 +145,6 @@
             pltpu.VMEM((faces, width, width), jnp.float32),
             pltpu.VMEM((faces, count, width), jnp.float32),
             pltpu.VMEM((faces, count, width), jnp.float32),
-            pltpu.VMEM((faces, count, count), jnp.float32),
         ],
         compiler_params=pltpu.CompilerParams(vmem_limit_bytes=60 * 1024 * 1024),
     )(*smem_args, *vmem_args)
@@ -155,14 +168,14 @@
     col = lax.broadcasted_iota(jnp.int32, (width, width), 1)
     axes = ("gx", "gy", "gz")
     packed_in = []
-    side_in = []
     for a in range(dims):
         halves = minus_local[a]
-        packed = jnp.where(col >= row, halves[:pairs], halves[pairs:])
+        packed = jnp.where(col >= row, halves[:pairs], halves[pairs:]).reshape(pairs * width, width)
         diagonals = jnp.sum(jnp.where(col == row, halves[pairs:], 0.0), axis=1)
-        side = jnp.concatenate([diagonals, jnp.broadcast_to(own_scale, (1, width))], axis=0)
-        packed_in.append(passed_along(packed, axes[a], -1))
-        side_in.append(passed_along(side, axes[a], -1))
+        scale_row = jnp.broadcast_to(own_scale, (1, width))
+        pad = jnp.zeros((-(pairs + 1) % 8, width), jnp.float32)
+        message = jnp.concatenate([packed, diagonals, scale_row, pad], axis=0)
+        packed_in.append(passed_along(message, axes[a], -1))
 
     scal = own_scale.reshape(1)
     n_inner = inner_local.shape[1]
@@ -171,7 +184,7 @@
     )
     cross_c, cross_e = run_faces(
         cross_kernel, dims * crossing, nsel, width, count, (scal, picks_flat),
-        (plus_local, *packed_in, *side_in, basis_vectors),
+        (plus_local, *packed_in, basis_vectors),
     )
     constraints = jnp.concatenate([cross_c, inner_c], axis=0)
     blocks = jnp.concatenate([cross_e, inner_e], axis=0)

time: 132 us -> 92.2 us (0.70)
  the two profiles are of different devices: /device:TPU:160 before, /device:TPU:6 now
where the time goes in v3:
time: 92.2 us; the launch traced here: 91.6 us
  Pallas kernels  47.2 us (51%)
  starting transfers between devices  20.8 us (23%)
  waiting for transfers between devices  11.1 us (12%)
  local copies, waits for them, and re-layouts  7.13 us (8%)
  other arithmetic  3.47 us (4%)
  between operations  1.53 us (2%)
    pallas_call x2, Pallas kernels, run_faces(): pl.pallas_call(kernel, out_shape=(jax.ShapeDtypeStruct((faces, nsel, widt...  47.2 us
    ppermute x3, starting transfers between devices, passed_along(): return lax.ppermute(block, axis, route)  11.9 us
    ppermute x3, waiting for transfers between devices, passed_along(): return lax.ppermute(block, axis, route)  10.4 us
    ppermute x7, starting transfers between devices, per_device(): coarse = coarse + lax.ppermute(part, 'gz', route)  8.89 us
    slice x1, local copies, waits for them, and re-layouts, per_device(): halves[:pairs]  2.36 us
    broadcast_in_dim x2, other arithmetic, per_device(): return (constraints[None, None, None], coarse[None, None])  2.18 us
  transfers between devices with their start and end apart: 10, of which 2 were waited for; matrix products, arithmetic and copies ran while one was open for 3% of the time, Pallas kernels for 23%

profile of v3, /device:TPU:6, one launch (start us, length us, event | category | flops | bytes accessed | tf_op | source)
XLA Modules:
  0.0 91.6 jit_solution(6412706722921525630)
XLA Ops:
  0.7 0.0 copy-start
  0.7 0.0 copy-start.7
  0.7 2.4 %fusion.18 = (f32[1,1,1,1,2,256,256]{6,5,4,3,2,1,0:T(8,128)S(1)}, f32[1,1,1,1,2,256,256]{6,5,4,3,2,1,0:T(8,128)S(1)}, f32[1,1,1,1,2,256,256]{6,5,4,3,2,1,0:T(8,1...) fusion(f32[1,1,1,3,4,256,256]{6,5,4,3,2,1,0:T(8,128)} %param.9), kind=kLoop, calls=%fused_computation.41 | loop fusion | bytes 6291456 | tf_op jit(solution)/shard_map/slice | solution.py:173
  3.1 0.4 copy-done
  3.5 0.1 fusion
  4.3 0.0 copy-done.7
  4.3 0.6 fusion.16
  5.0 0.7 pad.14.clone
  5.7 0.1 pad.15.clone
  5.7 0.0 copy-start.5
  5.7 0.2 bitcast_select_fusion
  6.0 0.2 maximum_maximum_fusion.2
  6.2 9.4 %collective-permute-start = (f32[520,256]{1,0:T(8,128)S(1)}, f32[520,256]{1,0:T(8,128)S(1)}, u32[]{:S(2)}, u32[]{:S(2)}) collective-permute-start(f32[520,256]{1,0:T(8,128)S(1)} %get-tuple-element.31), channel_id=1, source_target_pairs={{32,0},{64,32},{96,64},{128,96},{160,128},{192,160},{224,192},{33,... | collective-permute-start | bytes 1597448 | tf_op jit(solution)/shard_map/ppermute | solution.py:18
  15.6 1.3 %collective-permute-start.1 = (f32[520,256]{1,0:T(8,128)S(1)}, f32[520,256]{1,0:T(8,128)S(1)}, u32[]{:S(2)}, u32[]{:S(2)}) collective-permute-start(f32[520,256]{1,0:T(8,128)S(1)} %get-tuple-element.30), channel_id=1, source_target_pairs={{8,0},{16,8},{24,16},{9,1},{17,9},{25,17},{10,2},{18,10},{26,18},{... | collective-permute-start | bytes 1597448 | tf_op jit(solution)/shard_map/ppermute | solution.py:18
  16.9 1.3 %collective-permute-start.2 = (f32[520,256]{1,0:T(8,128)S(1)}, f32[520,256]{1,0:T(8,128)S(1)}, u32[]{:S(2)}, u32[]{:S(2)}) collective-permute-start(f32[520,256]{1,0:T(8,128)S(1)} %get-tuple-element.29), channel_id=1, source_target_pairs={{1,0},{2,1},{3,2},{4,3},{5,4},{6,5},{7,6},{9,8},{10,9},{11,10},{12... | collective-permute-start | bytes 1597448 | tf_op jit(solution)/shard_map/ppermute | solution.py:18
  18.3 0.0 copy-done.5
  18.3 0.1 copy.13
  18.4 0.7 reshape_squeeze.3.picks_ref
  19.0 20.9 %shard_map.96 = (f32[8,8,256]{2,1,0:T(8,128)}, f32[8,8,8]{2,1,0:T(8,128)}) custom-call(f32[1]{0:T(128)} %bitcast.1.scal_ref, s32[160]{0:T(256)} %reshape_squeeze.3.picks_ref, f32[2,8,256,256]{3,2,1,0:T(8,128)} %bitcast.75, f32[20,16,256]{2,1,0:T(8,128)} %bitcast.77), custom_call_target="tpu_custom_call" | custom-call | tf_op jit(solution)/shard_map/pallas_call | solution.py:135
  39.9 0.0 copy-start.6
  39.9 0.0 copy-start.4
  39.9 0.9 copy.15
  40.8 0.0 collective-permute-done.refs_0_
  40.8 0.0 copy-start.1
  40.8 10.4 %collective-permute-done.1.refs_1_ = f32[520,256]{1,0:T(8,128)S(1)} collective-permute-done((f32[520,256]{1,0:T(8,128)S(1)}, f32[520,256]{1,0:T(8,128)S(1)}, u32[]{:S(2)}, u32[]{:S(2)}) %collective-permute-start.1) | collective-permute-done | bytes 532512 | tf_op jit(solution)/shard_map/ppermute | solution.py:18
  51.2 0.0 copy-start.2
  51.2 0.0 collective-permute-done.2.refs_2_
  51.2 0.0 copy-start.3
  51.2 0.0 copy-done.1
  51.2 0.8 copy-done.2
  52.0 0.2 copy-done.3
  52.2 26.3 %shard_map.95 = (f32[12,8,256]{2,1,0:T(8,128)}, f32[12,8,8]{2,1,0:T(8,128)}) custom-call(f32[1]{0:T(128)} %bitcast.1.scal_ref, s32[160]{0:T(256)} %reshape_squeeze.3.picks_ref, f32[3,4,256,256]{3,2,1,0:T(8,128)} %bitcast.76, f32[520,256]{1,0:T(8,128)} %copy-done.1, f32[520,256]{1,0:T(8,128)} %copy-done.2, f32[520,256]{1,0:T(8,128)} %copy-done.3, ...), custom_call_target="tpu_custom_call" | custom-call | tf_op jit(solution)/shard_map/pallas_call | solution.py:135
  78.5 0.9 copy.14
  79.4 0.0 copy-done.6
  79.4 0.3 fusion.3
  79.7 0.0 collective-permute-start.3
  79.8 1.7 %collective-permute-start.4 = (f32[16,64]{1,0:T(8,128)S(1)}, f32[16,64]{1,0:T(8,128)S(1)}, u32[]{:S(2)}, u32[]{:S(2)}) collective-permute-start(f32[16,64]{1,0:T(8,128)S(1)} %get-tuple-element.25), channel_id=1, source_target_pairs={{0,2},{1,3},{2,4},{3,5},{4,6},{5,7},{6,0},{7,1},{8,10},{9,11},{10,... | collective-permute-start | bytes 12296 | tf_op jit(solution)/shard_map/ppermute | solution.py:201
  81.4 2.2 %collective-permute-start.5 = (f32[16,64]{1,0:T(8,128)S(1)}, f32[16,64]{1,0:T(8,128)S(1)}, u32[]{:S(2)}, u32[]{:S(2)}) collective-permute-start(f32[16,64]{1,0:T(8,128)S(1)} %get-tuple-element.24), channel_id=1, source_target_pairs={{0,3},{1,4},{2,5},{3,6},{4,7},{5,0},{6,1},{7,2},{8,11},{9,12},{10,... | collective-permute-start | bytes 12296 | tf_op jit(solution)/shard_map/ppermute | solution.py:201
  83.6 1.8 %collective-permute-start.6 = (f32[16,64]{1,0:T(8,128)S(1)}, f32[16,64]{1,0:T(8,128)S(1)}, u32[]{:S(2)}, u32[]{:S(2)}) collective-permute-start(f32[16,64]{1,0:T(8,128)S(1)} %get-tuple-element.23), channel_id=1, source_target_pairs={{0,4},{1,5},{2,6},{3,7},{4,0},{5,1},{6,2},{7,3},{8,12},{9,13},{10,... | collective-permute-start | bytes 12296 | tf_op jit(solution)/shard_map/ppermute | solution.py:201
  85.5 1.8 %collective-permute-start.7 = (f32[16,64]{1,0:T(8,128)S(1)}, f32[16,64]{1,0:T(8,128)S(1)}, u32[]{:S(2)}, u32[]{:S(2)}) collective-permute-start(f32[16,64]{1,0:T(8,128)S(1)} %get-tuple-element.22), channel_id=1, source_target_pairs={{0,5},{1,6},{2,7},{3,0},{4,1},{5,2},{6,3},{7,4},{8,13},{9,14},{10,... | collective-permute-start | bytes 12296 | tf_op jit(solution)/shard_map/ppermute | solution.py:201
  87.3 0.0 collective-permute-done.3
  87.3 1.3 %collective-permute-start.8 = (f32[16,64]{1,0:T(8,128)S(1)}, f32[16,64]{1,0:T(8,128)S(1)}, u32[]{:S(2)}, u32[]{:S(2)}) collective-permute-start(f32[16,64]{1,0:T(8,128)S(1)} %get-tuple-element.21), channel_id=1, source_target_pairs={{0,6},{1,7},{2,0},{3,1},{4,2},{5,3},{6,4},{7,5},{8,14},{9,15},{10,... | collective-permute-start | bytes 12296 | tf_op jit(solution)/shard_map/ppermute | solution.py:201
  88.6 0.0 collective-permute-done.4
  88.6 0.0 collective-permute-start.9
  88.6 0.0 copy-done.4
  88.7 1.6 %maximum_bitcast_fusion = f32[1,1,1,20,8,256]{5,4,3,2,1,0:T(8,128)} fusion(f32[8,8,256]{2,1,0:T(8,128)S(1)} %copy-done.4, f32[12,8,256]{2,1,0:T(8,128)} %get-tuple-element.6), kind=kLoop, calls=%fused_computation.14 | loop fusion | flops 40960 | bytes 327680 | tf_op jit(solution)/shard_map/broadcast_in_dim | solution.py:202
  90.2 0.0 collective-permute-done.5
  90.2 0.0 collective-permute-done.6
  90.2 0.0 collective-permute-done.7
  90.2 0.7 collective-permute-done.8
  90.9 0.0 collective-permute-done.9
  90.9 0.6 fusion.15
  (5 shorter events, 0.1 us)
Async XLA Ops:
  0.7 2.8 %copy-start = (f32[1,1,1,3,4,256,256]{6,5,4,3,2,1,0:T(8,128)S(1)}, f32[1,1,1,3,4,256,256]{6,5,4,3,2,1,0:T(8,128)}, u32[]{:S(2)}) copy-start(f32[1,1,1,3,4,256,256]{6,5,4,3,2,1,0:T(8,128)} %param.9) | copy-start | bytes 9437188
  0.7 3.6 %copy-start.7 = (f32[4]{0:T(128)S(1)}, f32[4]{0:T(128)}, u32[]{:S(2)}) copy-start(f32[4]{0:T(128)} %param.15) | copy-start | bytes 52
  5.7 12.5 %copy-start.5 = (s32[1,1,1,20,8]{3,4,2,1,0:T(8,128)S(1)}, s32[1,1,1,20,8]{3,4,2,1,0:T(8,128)}, u32[]{:S(2)}) copy-start(s32[1,1,1,20,8]{3,4,2,1,0:T(8,128)} %param.12) | copy-start | bytes 1924
  6.2 34.6 %collective-permute-start = (f32[520,256]{1,0:T(8,128)S(1)}, f32[520,256]{1,0:T(8,128)S(1)}, u32[]{:S(2)}, u32[]{:S(2)}) collective-permute-start(f32[520,256]{1,0:T(8,128)S(1)} %get-tuple-element.31), channel_id=1, source_target_pairs={{32,0},{64,32},{96,64},{128,96},{160,128},{192,160},{224,192},{33,... | collective-permute-start | bytes 1597448 | tf_op jit(solution)/shard_map/ppermute | solution.py:18
  15.6 35.6 %collective-permute-start.1 = (f32[520,256]{1,0:T(8,128)S(1)}, f32[520,256]{1,0:T(8,128)S(1)}, u32[]{:S(2)}, u32[]{:S(2)}) collective-permute-start(f32[520,256]{1,0:T(8,128)S(1)} %get-tuple-element.30), channel_id=1, source_target_pairs={{8,0},{16,8},{24,16},{9,1},{17,9},{25,17},{10,2},{18,10},{26,18},{... | collective-permute-start | bytes 1597448 | tf_op jit(solution)/shard_map/ppermute | solution.py:18
  16.9 34.3 %collective-permute-start.2 = (f32[520,256]{1,0:T(8,128)S(1)}, f32[520,256]{1,0:T(8,128)S(1)}, u32[]{:S(2)}, u32[]{:S(2)}) collective-permute-start(f32[520,256]{1,0:T(8,128)S(1)} %get-tuple-element.29), channel_id=1, source_target_pairs={{1,0},{2,1},{3,2},{4,3},{5,4},{6,5},{7,6},{9,8},{10,9},{11,10},{12... | collective-permute-start | bytes 1597448 | tf_op jit(solution)/shard_map/ppermute | solution.py:18
  39.9 39.5 %copy-start.6 = (s32[1,1,1,20]{3,2,1,0:T(1,128)S(1)}, s32[1,1,1,20]{3,2,1,0:T(1,128)}, u32[]{:S(2)}) copy-start(s32[1,1,1,20]{3,2,1,0:T(1,128)} %param.13) | copy-start | bytes 244
  39.9 48.7 %copy-start.4 = (f32[8,8,256]{2,1,0:T(8,128)S(1)}, f32[8,8,256]{2,1,0:T(8,128)}, u32[]{:S(2)}) copy-start(f32[8,8,256]{2,1,0:T(8,128)} %get-tuple-element.7) | copy-start | bytes 196612
  40.8 10.4 %copy-start.1 = (f32[520,256]{1,0:T(8,128)}, f32[520,256]{1,0:T(8,128)S(1)}, u32[]{:S(2)}) copy-start(f32[520,256]{1,0:T(8,128)S(1)} %collective-permute-done.refs_0_) | copy-start | bytes 1597444
  51.2 0.8 copy-start.2
  51.2 1.0 %copy-start.3 = (f32[520,256]{1,0:T(8,128)}, f32[520,256]{1,0:T(8,128)S(1)}, u32[]{:S(2)}) copy-start(f32[520,256]{1,0:T(8,128)S(1)} %collective-permute-done.2.refs_2_) | copy-start | bytes 1597444
  79.7 7.6 %collective-permute-start.3 = (f32[16,64]{1,0:T(8,128)S(1)}, f32[16,64]{1,0:T(8,128)S(1)}, u32[]{:S(2)}, u32[]{:S(2)}) collective-permute-start(f32[16,64]{1,0:T(8,128)S(1)} %get-tuple-element.19), channel_id=1, source_target_pairs={{0,1},{1,2},{2,3},{3,4},{4,5},{5,6},{6,7},{7,0},{8,9},{9,10},{10,1... | collective-permute-start | bytes 12296 | tf_op jit(solution)/shard_map/ppermute | solution.py:201
  79.8 8.9 %collective-permute-start.4 = (f32[16,64]{1,0:T(8,128)S(1)}, f32[16,64]{1,0:T(8,128)S(1)}, u32[]{:S(2)}, u32[]{:S(2)}) collective-permute-start(f32[16,64]{1,0:T(8,128)S(1)} %get-tuple-element.25), channel_id=1, source_target_pairs={{0,2},{1,3},{2,4},{3,5},{4,6},{5,7},{6,0},{7,1},{8,10},{9,11},{10,... | collective-permute-start | bytes 12296 | tf_op jit(solution)/shard_map/ppermute | solution.py:201
  81.4 8.8 %collective-permute-start.5 = (f32[16,64]{1,0:T(8,128)S(1)}, f32[16,64]{1,0:T(8,128)S(1)}, u32[]{:S(2)}, u32[]{:S(2)}) collective-permute-start(f32[16,64]{1,0:T(8,128)S(1)} %get-tuple-element.24), channel_id=1, source_target_pairs={{0,3},{1,4},{2,5},{3,6},{4,7},{5,0},{6,1},{7,2},{8,11},{9,12},{10,... | collective-permute-start | bytes 12296 | tf_op jit(solution)/shard_map/ppermute | solution.py:201
  83.6 6.6 %collective-permute-start.6 = (f32[16,64]{1,0:T(8,128)S(1)}, f32[16,64]{1,0:T(8,128)S(1)}, u32[]{:S(2)}, u32[]{:S(2)}) collective-permute-start(f32[16,64]{1,0:T(8,128)S(1)} %get-tuple-element.23), channel_id=1, source_target_pairs={{0,4},{1,5},{2,6},{3,7},{4,0},{5,1},{6,2},{7,3},{8,12},{9,13},{10,... | collective-permute-start | bytes 12296 | tf_op jit(solution)/shard_map/ppermute | solution.py:201
  85.5 4.8 %collective-permute-start.7 = (f32[16,64]{1,0:T(8,128)S(1)}, f32[16,64]{1,0:T(8,128)S(1)}, u32[]{:S(2)}, u32[]{:S(2)}) collective-permute-start(f32[16,64]{1,0:T(8,128)S(1)} %get-tuple-element.22), channel_id=1, source_target_pairs={{0,5},{1,6},{2,7},{3,0},{4,1},{5,2},{6,3},{7,4},{8,13},{9,14},{10,... | collective-permute-start | bytes 12296 | tf_op jit(solution)/shard_map/ppermute | solution.py:201
  87.3 3.7 %collective-permute-start.8 = (f32[16,64]{1,0:T(8,128)S(1)}, f32[16,64]{1,0:T(8,128)S(1)}, u32[]{:S(2)}, u32[]{:S(2)}) collective-permute-start(f32[16,64]{1,0:T(8,128)S(1)} %get-tuple-element.21), channel_id=1, source_target_pairs={{0,6},{1,7},{2,0},{3,1},{4,2},{5,3},{6,4},{7,5},{8,14},{9,15},{10,... | collective-permute-start | bytes 12296 | tf_op jit(solution)/shard_map/ppermute | solution.py:201
  88.6 2.3 %collective-permute-start.9 = (f32[16,64]{1,0:T(8,128)S(1)}, f32[16,64]{1,0:T(8,128)S(1)}, u32[]{:S(2)}, u32[]{:S(2)}) collective-permute-start(f32[16,64]{1,0:T(8,128)S(1)} %get-tuple-element.20), channel_id=1, source_target_pairs={{0,7},{1,0},{2,1},{3,2},{4,3},{5,4},{6,5},{7,6},{8,15},{9,8},{10,9... | collective-permute-start | bytes 12296 | tf_op jit(solution)/shard_map/ppermute | solution.py:201

commit v4 on v3

--- a/solution.py
+++ b/solution.py
@@ -1,3 +1,4 @@
+import functools
 import math
 
 import jax
@@ -50,7 +51,7 @@
     return [item[1].reshape(item[1].shape[0] * count, -1) for item in state]
 
 
-def iterate(own, picks_ref, pick_base, c_ref, e_ref, m_scr, v_scr, w_scr):
+def iterate(own, picks_ref, first, c_ref, e_ref, m_scr, v_scr, w_scr):
     faces, count = v_scr.shape[0], v_scr.shape[1]
     nsel = c_ref.shape[1]
     scale_out = math.sqrt(m_scr.shape[-1])
@@ -75,27 +76,17 @@
             v_scr[g0:g1] = solved.reshape(g1 - g0, count, -1)
 
     def finish(f, carry):
-        rows = [v_scr[f, pl.ds(picks_ref[pick_base + f * nsel + s], 1), :] for s in range(nsel)]
+        rows = [v_scr[f, pl.ds(picks_ref[(first + f) * nsel + s], 1), :] for s in range(nsel)]
         picked = jnp.concatenate(rows, axis=0)
-        c_ref[f] = picked * scale_out
+        c_ref[first + f] = picked * scale_out
         images = jnp.dot(picked, m_scr[f], precision=HIGHEST, preferred_element_type=jnp.float32)
         block = lax.dot_general(
             picked, images, (((1,), (1,)), ((), ())), precision=HIGHEST, preferred_element_type=jnp.float32
         )
-        e_ref[f] = block / own
+        e_ref[first + f] = block / own
         return carry
 
     lax.fori_loop(0, faces, finish, 0, unroll=2)
-
-
-def inner_kernel(scal_ref, picks_ref, inner_ref, v0_ref, c_ref, e_ref, m_scr, v_scr, w_scr):
-    faces = m_scr.shape[0]
-    base = v0_ref.shape[0] - faces
-    own = scal_ref[0]
-    for f in range(faces):
-        m_scr[f] = own * inner_ref[0, f] + own * inner_ref[1, f]
-        v_scr[f] = v0_ref[base + f]
-    iterate(own, picks_ref, base * c_ref.shape[1], c_ref, e_ref, m_scr, v_scr, w_scr)
 
 
 def unpacked(packed, side, index, pairs):
@@ -111,43 +102,59 @@
     return jnp.where(col > row, turned, jnp.where(col == row, diagonal, mixed))
 
 
-def cross_kernel(scal_ref, picks_ref, plus_ref, *refs):
-    dims = plus_ref.shape[0]
-    packed_refs = refs[:dims]
-    v0_ref, c_ref, e_ref, m_scr, v_scr, w_scr = refs[dims:]
+def face_kernel(cross_axes, with_inner, scal_ref, picks_ref, plus_ref, *refs):
+    packed_refs = refs[: len(cross_axes)]
+    rest = refs[len(cross_axes) :]
+    inner_ref = rest[0] if with_inner else None
+    rest = rest[1:] if with_inner else rest
+    v0_ref = rest[0]
+    c_ref, e_ref, m_scr, v_scr, w_scr = rest[-5:]
+    if len(rest) > 6:
+        c_ref[...] = rest[1][...]
+        e_ref[...] = rest[2][...]
     crossing, width = plus_ref.shape[1], plus_ref.shape[-1]
     pairs = crossing // 2
+    first = cross_axes[0] * crossing
     own = scal_ref[0]
-    for a in range(dims):
-        packed = packed_refs[a]
+    f = 0
+    for a, packed in zip(cross_axes, packed_refs):
         side = packed[pairs * width :, :]
         next_scale = side[pairs : pairs + 1, 0:1]
         for k in range(crossing):
-            f = a * crossing + k
             m_scr[f] = own * plus_ref[a, k] + next_scale * unpacked(packed, side, k, pairs)
-            v_scr[f] = v0_ref[f]
-    iterate(own, picks_ref, 0, c_ref, e_ref, m_scr, v_scr, w_scr)
-
-
-def run_faces(kernel, faces, nsel, width, count, smem_args, vmem_args):
+            v_scr[f] = v0_ref[first + f]
+            f += 1
+    if with_inner:
+        for k in range(inner_ref.shape[1]):
+            m_scr[f] = own * inner_ref[0, k] + own * inner_ref[1, k]
+            v_scr[f] = v0_ref[first + f]
+            f += 1
+    iterate(own, picks_ref, first, c_ref, e_ref, m_scr, v_scr, w_scr)
+
+
+def run_faces(kernel, faces, nsel, width, count, smem_args, vmem_args, earlier=()):
     vmem = pltpu.MemorySpace.VMEM
     smem = pltpu.MemorySpace.SMEM
+    total = vmem_args[-1].shape[0]
+    args = (*smem_args, *vmem_args, *earlier)
+    aliases = {len(args) - len(earlier) + i: i for i in range(len(earlier))}
     return pl.pallas_call(
         kernel,
         out_shape=(
-            jax.ShapeDtypeStruct((faces, nsel, width), jnp.float32),
-            jax.ShapeDtypeStruct((faces, nsel, nsel), jnp.float32),
+            jax.ShapeDtypeStruct((total, nsel, width), jnp.float32),
+            jax.ShapeDtypeStruct((total, nsel, nsel), jnp.float32),
         ),
         in_specs=[pl.BlockSpec(memory_space=smem)] * len(smem_args)
-        + [pl.BlockSpec(memory_space=vmem)] * len(vmem_args),
+        + [pl.BlockSpec(memory_space=vmem)] * (len(vmem_args) + len(earlier)),
         out_specs=(pl.BlockSpec(memory_space=vmem), pl.BlockSpec(memory_space=vmem)),
         scratch_shapes=[
             pltpu.VMEM((faces, width, width), jnp.float32),
             pltpu.VMEM((faces, count, width), jnp.float32),
             pltpu.VMEM((faces, count, width), jnp.float32),
         ],
+        input_output_aliases=aliases,
         compiler_params=pltpu.CompilerParams(vmem_limit_bytes=60 * 1024 * 1024),
-    )(*smem_args, *vmem_args)
+    )(*args)
 
 
 def per_device(
@@ -179,26 +186,21 @@
 
     scal = own_scale.reshape(1)
     n_inner = inner_local.shape[1]
-    inner_c, inner_e = run_faces(
-        inner_kernel, n_inner, nsel, width, count, (scal, picks_flat), (inner_local, basis_vectors)
+    late = tuple(range(dims - 1))
+    early_c, early_e = run_faces(
+        functools.partial(face_kernel, (dims - 1,), True), crossing + n_inner, nsel, width, count,
+        (scal, picks_flat), (plus_local, packed_in[dims - 1], inner_local, basis_vectors),
     )
-    cross_c, cross_e = run_faces(
-        cross_kernel, dims * crossing, nsel, width, count, (scal, picks_flat),
-        (plus_local, *packed_in, basis_vectors),
+    constraints, blocks = run_faces(
+        functools.partial(face_kernel, late, False), len(late) * crossing, nsel, width, count,
+        (scal, picks_flat), (plus_local, *packed_in[: dims - 1], basis_vectors), (early_c, early_e),
     )
-    constraints = jnp.concatenate([cross_c, inner_c], axis=0)
-    blocks = jnp.concatenate([cross_e, inner_e], axis=0)
     flat = blocks.reshape(faces_all, -1)
     groups = lax.axis_size("gz")
     rows_all = groups * CROWS
     owner_hot = (owner[0, 0, 0][:, None] == jnp.arange(rows_all, dtype=jnp.int32)).astype(jnp.float32)
     term = jnp.einsum("fr,fe->re", owner_hot, flat, precision=HIGHEST).reshape(groups, CROWS, -1)
-    me = lax.axis_index("gz")
-    coarse = lax.dynamic_index_in_dim(term, me, 0, keepdims=False)
-    for shift in range(1, groups):
-        part = lax.dynamic_index_in_dim(term, (me + shift) % groups, 0, keepdims=False)
-        route = [(i, (i + shift) % groups) for i in range(groups)]
-        coarse = coarse + lax.ppermute(part, "gz", route)
+    coarse = jnp.sum(lax.all_to_all(term, "gz", 0, 0), axis=0)
     return (constraints[None, None, None], coarse[None, None])
 
 

time: 92.2 us -> 89.3 us (0.969)
  blocking collectives: 0 us -> 10 us
  starting transfers between devices: 20.8 us -> 11.9 us
  waiting for transfers between devices: 11.1 us -> 6.65 us
  Pallas kernels: 47.2 us -> 48.5 us
    all_to_all x0 -> x1, blocking collectives: none -> 10 us  [per_device(): coarse = jnp.sum(lax.all_to_all(term, 'gz', 0, 0), axis=0)]
    ppermute x7 -> x0, starting transfers between devices: 8.89 us -> none  [per_device(): coarse = coarse + lax.ppermute(part, 'gz', route)]
    ppermute x3, waiting for transfers between devices: 10.4 us -> 6.65 us  [passed_along(): return lax.ppermute(block, axis, route)]
    broadcast_in_dim x2 -> x0, other arithmetic: 2.18 us -> none  [per_device(): return (constraints[None, None, None], coarse[None, None])]
    pallas_call x2, Pallas kernels: 47.2 us -> 48.5 us  [run_faces(): pl.pallas_call(kernel, out_shape=(jax.ShapeDtypeStruct((total, nsel, widt...]
  transfers between devices with their start and end apart: 10 -> 3, of which waited for: 2 -> 1; matrix products, arithmetic and copies ran while one was open for 3% -> 1% of each run, Pallas kernels for 23% -> 30%
where the time goes in v4:
time: 89.3 us; the launch traced here: 89 us
  Pallas kernels  48.5 us (54%)
  starting transfers between devices  11.9 us (13%)
  blocking collectives  10 us (11%)
  local copies, waits for them, and re-layouts  7.63 us (9%)
  waiting for transfers between devices  6.65 us (7%)
  other arithmetic  2.61 us (3%)
  between operations  1.41 us (2%)
    pallas_call x2, Pallas kernels, run_faces(): pl.pallas_call(kernel, out_shape=(jax.ShapeDtypeStruct((total, nsel, widt...  48.5 us
    ppermute x3, starting transfers between devices, passed_along(): return lax.ppermute(block, axis, route)  11.9 us
    all_to_all x1, blocking collectives, per_device(): coarse = jnp.sum(lax.all_to_all(term, 'gz', 0, 0), axis=0)  10 us
    ppermute x3, waiting for transfers between devices, passed_along(): return lax.ppermute(block, axis, route)  6.65 us
    slice x1, local copies, waits for them, and re-layouts, per_device(): halves[:pairs]  2.36 us
    unnamed x17, local copies, waits for them, and re-layouts  2.32 us
  transfers between devices with their start and end apart: 3, of which 1 were waited for; matrix products, arithmetic and copies ran while one was open for 1% of the time, Pallas kernels for 30%

profile of v4, /device:TPU:6, one launch (start us, length us, event | category | flops | bytes accessed | tf_op | source)
XLA Modules:
  0.0 89.0 jit_solution(5104031029436902107)
XLA Ops:
  0.7 0.0 copy-start
  0.7 0.0 copy-start.6
  0.7 2.4 %fusion.9 = (f32[1,1,1,1,2,256,256]{6,5,4,3,2,1,0:T(8,128)S(1)}, f32[1,1,1,1,2,256,256]{6,5,4,3,2,1,0:T(8,128)S(1)}, f32[1,1,1,1,2,256,256]{6,5,4,3,2,1,0:T(8,12...) fusion(f32[1,1,1,3,4,256,256]{6,5,4,3,2,1,0:T(8,128)} %param.9), kind=kLoop, calls=%fused_computation.22 | loop fusion | bytes 6291456 | tf_op jit(solution)/shard_map/slice | solution.py:180
  3.1 0.4 copy-done
  3.5 0.1 fusion
  4.3 0.0 copy-done.6
  4.3 0.6 fusion.8
  5.0 0.7 pad.10.clone
  5.7 0.1 pad.11.clone
  5.7 0.0 copy-start.4
  5.8 0.2 bitcast_select_fusion
  6.0 0.2 maximum_maximum_fusion.2
  6.2 1.3 %collective-permute-start.2 = (f32[520,256]{1,0:T(8,128)S(1)}, f32[520,256]{1,0:T(8,128)S(1)}, u32[]{:S(2)}, u32[]{:S(2)}) collective-permute-start(f32[520,256]{1,0:T(8,128)S(1)} %get-tuple-element.22), channel_id=1, source_target_pairs={{1,0},{2,1},{3,2},{4,3},{5,4},{6,5},{7,6},{9,8},{10,9},{11,10},{12... | collective-permute-start | bytes 1597448 | tf_op jit(solution)/shard_map/ppermute | solution.py:19
  7.5 9.4 %collective-permute-start = (f32[520,256]{1,0:T(8,128)S(1)}, f32[520,256]{1,0:T(8,128)S(1)}, u32[]{:S(2)}, u32[]{:S(2)}) collective-permute-start(f32[520,256]{1,0:T(8,128)S(1)} %get-tuple-element.24), channel_id=1, source_target_pairs={{32,0},{64,32},{96,64},{128,96},{160,128},{192,160},{224,192},{33,... | collective-permute-start | bytes 1597448 | tf_op jit(solution)/shard_map/ppermute | solution.py:19
  16.9 1.3 %collective-permute-start.1 = (f32[520,256]{1,0:T(8,128)S(1)}, f32[520,256]{1,0:T(8,128)S(1)}, u32[]{:S(2)}, u32[]{:S(2)}) collective-permute-start(f32[520,256]{1,0:T(8,128)S(1)} %get-tuple-element.23), channel_id=1, source_target_pairs={{8,0},{16,8},{24,16},{9,1},{17,9},{25,17},{10,2},{18,10},{26,18},{... | collective-permute-start | bytes 1597448 | tf_op jit(solution)/shard_map/ppermute | solution.py:19
  18.2 0.0 copy-done.4
  18.2 0.1 copy.12
  18.3 0.7 reshape_squeeze.3.picks_ref
  18.9 0.0 collective-permute-done.2.refs_0_
  18.9 0.0 copy-start.1
  18.9 0.8 copy-done.1
  19.7 27.1 %shard_map.95 = (f32[20,8,256]{2,1,0:T(8,128)}, f32[20,8,8]{2,1,0:T(8,128)}) custom-call(f32[1]{0:T(128)} %bitcast.1.scal_ref, s32[160]{0:T(256)} %reshape_squeeze.3.picks_ref, f32[3,4,256,256]{3,2,1,0:T(8,128)} %bitcast.43, f32[520,256]{1,0:T(8,128)} %copy-done.1, f32[2,8,256,256]{3,2,1,0:T(8,128)} %bitcast.45, f32[20,16,256]{2,1,0:T(8,128)} %bitcast.46), custom_call_target="tpu_custom_call" | custom-call | tf_op jit(solution)/shard_map/pallas_call | solution.py:141
  46.8 0.0 copy-start.5
  46.8 0.0 collective-permute-done.refs_0_
  46.8 0.0 copy-start.2
  46.9 6.6 %collective-permute-done.1.refs_1_ = f32[520,256]{1,0:T(8,128)S(1)} collective-permute-done((f32[520,256]{1,0:T(8,128)S(1)}, f32[520,256]{1,0:T(8,128)S(1)}, u32[]{:S(2)}, u32[]{:S(2)}) %collective-permute-start.1) | collective-permute-done | bytes 532512 | tf_op jit(solution)/shard_map/ppermute | solution.py:19
  53.5 0.0 copy-start.3
  53.5 0.0 copy-done.2
  53.5 0.8 copy-done.3
  54.3 21.4 %shard_map.96 = (f32[20,8,256]{2,1,0:T(8,128)}, f32[20,8,8]{2,1,0:T(8,128)}) custom-call(f32[1]{0:T(128)} %bitcast.1.scal_ref, s32[160]{0:T(256)} %reshape_squeeze.3.picks_ref, f32[3,4,256,256]{3,2,1,0:T(8,128)} %bitcast.44, f32[520,256]{1,0:T(8,128)} %copy-done.2, f32[520,256]{1,0:T(8,128)} %copy-done.3, ...), custom_call_target="tpu_custom_call", output_to_operand_aliasing={{0}: (6, {}), {1}: (7, {})} | custom-call | tf_op jit(solution)/shard_map/pallas_call | solution.py:141
  75.7 1.0 %copy.13 = f32[20,8,8]{0,2,1:T(8,128)S(1)} copy(f32[20,8,8]{2,1,0:T(8,128)} %get-tuple-element.9) | data formatting | bytes 10240 | tf_op jit(solution)/shard_map/pallas_call | solution.py:141
  76.7 0.0 copy-done.5
  76.7 0.2 fusion.3
  77.0 0.1 reshape.62
  77.1 10.0 %all_to_all.5 = f32[8,1,1024]{2,1,0:T(1,128)S(1)} all-to-all(f32[8,1,1024]{2,1,0:T(1,128)S(1)} %reshape.62), channel_id=1, replica_groups=mesh['gx'=8,'gy'=4,'gz'=8] {'gz'}, dimensions={0} | all-to-all | bytes 65536 | tf_op jit(solution)/shard_map/all_to_all | solution.py:203
  87.1 0.5 broadcast.35
  87.6 0.7 reduce
  88.3 0.1 reshape.63
  88.4 0.6 reduce_sum.49
  (4 shorter events, 0.1 us)
Async XLA Ops:
  0.7 2.8 %copy-start = (f32[1,1,1,3,4,256,256]{6,5,4,3,2,1,0:T(8,128)S(1)}, f32[1,1,1,3,4,256,256]{6,5,4,3,2,1,0:T(8,128)}, u32[]{:S(2)}) copy-start(f32[1,1,1,3,4,256,256]{6,5,4,3,2,1,0:T(8,128)} %param.9) | copy-start | bytes 9437188
  0.7 3.6 %copy-start.6 = (f32[4]{0:T(128)S(1)}, f32[4]{0:T(128)}, u32[]{:S(2)}) copy-start(f32[4]{0:T(128)} %param.15) | copy-start | bytes 52
  5.7 12.4 %copy-start.4 = (s32[1,1,1,20,8]{3,4,2,1,0:T(8,128)S(1)}, s32[1,1,1,20,8]{3,4,2,1,0:T(8,128)}, u32[]{:S(2)}) copy-start(s32[1,1,1,20,8]{3,4,2,1,0:T(8,128)} %param.12) | copy-start | bytes 1924
  6.2 12.7 %collective-permute-start.2 = (f32[520,256]{1,0:T(8,128)S(1)}, f32[520,256]{1,0:T(8,128)S(1)}, u32[]{:S(2)}, u32[]{:S(2)}) collective-permute-start(f32[520,256]{1,0:T(8,128)S(1)} %get-tuple-element.22), channel_id=1, source_target_pairs={{1,0},{2,1},{3,2},{4,3},{5,4},{6,5},{7,6},{9,8},{10,9},{11,10},{12... | collective-permute-start | bytes 1597448 | tf_op jit(solution)/shard_map/ppermute | solution.py:19
  7.5 39.3 %collective-permute-start = (f32[520,256]{1,0:T(8,128)S(1)}, f32[520,256]{1,0:T(8,128)S(1)}, u32[]{:S(2)}, u32[]{:S(2)}) collective-permute-start(f32[520,256]{1,0:T(8,128)S(1)} %get-tuple-element.24), channel_id=1, source_target_pairs={{32,0},{64,32},{96,64},{128,96},{160,128},{192,160},{224,192},{33,... | collective-permute-start | bytes 1597448 | tf_op jit(solution)/shard_map/ppermute | solution.py:19
  16.9 36.6 %collective-permute-start.1 = (f32[520,256]{1,0:T(8,128)S(1)}, f32[520,256]{1,0:T(8,128)S(1)}, u32[]{:S(2)}, u32[]{:S(2)}) collective-permute-start(f32[520,256]{1,0:T(8,128)S(1)} %get-tuple-element.23), channel_id=1, source_target_pairs={{8,0},{16,8},{24,16},{9,1},{17,9},{25,17},{10,2},{18,10},{26,18},{... | collective-permute-start | bytes 1597448 | tf_op jit(solution)/shard_map/ppermute | solution.py:19
  18.9 0.8 copy-start.1
  46.8 29.9 %copy-start.5 = (s32[1,1,1,20]{3,2,1,0:T(1,128)S(1)}, s32[1,1,1,20]{3,2,1,0:T(1,128)}, u32[]{:S(2)}) copy-start(s32[1,1,1,20]{3,2,1,0:T(1,128)} %param.13) | copy-start | bytes 244
  46.8 6.7 %copy-start.2 = (f32[520,256]{1,0:T(8,128)}, f32[520,256]{1,0:T(8,128)S(1)}, u32[]{:S(2)}) copy-start(f32[520,256]{1,0:T(8,128)S(1)} %collective-permute-done.refs_0_) | copy-start | bytes 1597444
  53.5 0.8 copy-start.3

commit v5 on v4

--- a/solution.py
+++ b/solution.py
@@ -58,7 +58,7 @@
     spans = [(g, min(g + GROUP, faces)) for g in range(0, faces, GROUP)]
 
     def image(f, carry):
-        w_scr[f] = jnp.dot(v_scr[f], m_scr[f], precision=HIGHEST, preferred_element_type=jnp.float32)
+        w_scr[f] = jnp.dot(v_scr[f], m_scr[f], precision=lax.Precision.HIGH, preferred_element_type=jnp.float32)
         return carry
 
     for iteration in range(ITERS):

time: 89.3 us -> 87.6 us (0.981)
  Pallas kernels: 48.5 us -> 44.2 us
  waiting for transfers between devices: 6.65 us -> 9.25 us
    pallas_call x2, Pallas kernels: 48.5 us -> 44.2 us  [run_faces(): pl.pallas_call(kernel, out_shape=(jax.ShapeDtypeStruct((total, nsel, widt...]
    ppermute x3, waiting for transfers between devices: 6.65 us -> 9.25 us  [passed_along(): return lax.ppermute(block, axis, route)]
  transfers between devices with their start and end apart: 3 -> 3, of which waited for: 1 -> 1; matrix products, arithmetic and copies ran while one was open for 1% -> 1% of each run, Pallas kernels for 30% -> 28%
where the time goes in v5:
time: 87.6 us; the launch traced here: 87.3 us
  Pallas kernels  44.2 us (50%)
  starting transfers between devices  11.9 us (14%)
  blocking collectives  10 us (11%)
  waiting for transfers between devices  9.25 us (11%)
  local copies, waits for them, and re-layouts  7.63 us (9%)
  other arithmetic  2.61 us (3%)
  between operations  1.41 us (2%)
    pallas_call x2, Pallas kernels, run_faces(): pl.pallas_call(kernel, out_shape=(jax.ShapeDtypeStruct((total, nsel, widt...  44.2 us
    ppermute x3, starting transfers between devices, passed_along(): return lax.ppermute(block, axis, route)  11.9 us
    all_to_all x1, blocking collectives, per_device(): coarse = jnp.sum(lax.all_to_all(term, 'gz', 0, 0), axis=0)  10 us
    ppermute x3, waiting for transfers between devices, passed_along(): return lax.ppermute(block, axis, route)  9.25 us
    slice x1, local copies, waits for them, and re-layouts, per_device(): halves[:pairs]  2.36 us
    unnamed x17, local copies, waits for them, and re-layouts  2.32 us
  transfers between devices with their start and end apart: 3, of which 1 were waited for; matrix products, arithmetic and copies ran while one was open for 1% of the time, Pallas kernels for 28%

profile of v5, /device:TPU:6, one launch (start us, length us, event | category | flops | bytes accessed | tf_op | source)
XLA Modules:
  0.0 87.3 jit_solution(1269544550138373503)
XLA Ops:
  0.7 0.0 copy-start
  0.7 0.0 copy-start.6
  0.7 2.4 %fusion.9 = (f32[1,1,1,1,2,256,256]{6,5,4,3,2,1,0:T(8,128)S(1)}, f32[1,1,1,1,2,256,256]{6,5,4,3,2,1,0:T(8,128)S(1)}, f32[1,1,1,1,2,256,256]{6,5,4,3,2,1,0:T(8,12...) fusion(f32[1,1,1,3,4,256,256]{6,5,4,3,2,1,0:T(8,128)} %param.9), kind=kLoop, calls=%fused_computation.22 | loop fusion | bytes 6291456 | tf_op jit(solution)/shard_map/slice | solution.py:180
  3.1 0.4 copy-done
  3.5 0.1 fusion
  4.3 0.0 copy-done.6
  4.3 0.6 fusion.8
  5.0 0.7 pad.10.clone
  5.7 0.1 pad.11.clone
  5.7 0.0 copy-start.4
  5.8 0.2 bitcast_select_fusion
  6.0 0.2 maximum_maximum_fusion.2
  6.2 1.3 %collective-permute-start.2 = (f32[520,256]{1,0:T(8,128)S(1)}, f32[520,256]{1,0:T(8,128)S(1)}, u32[]{:S(2)}, u32[]{:S(2)}) collective-permute-start(f32[520,256]{1,0:T(8,128)S(1)} %get-tuple-element.22), channel_id=1, source_target_pairs={{1,0},{2,1},{3,2},{4,3},{5,4},{6,5},{7,6},{9,8},{10,9},{11,10},{12... | collective-permute-start | bytes 1597448 | tf_op jit(solution)/shard_map/ppermute | solution.py:19
  7.5 9.4 %collective-permute-start = (f32[520,256]{1,0:T(8,128)S(1)}, f32[520,256]{1,0:T(8,128)S(1)}, u32[]{:S(2)}, u32[]{:S(2)}) collective-permute-start(f32[520,256]{1,0:T(8,128)S(1)} %get-tuple-element.24), channel_id=1, source_target_pairs={{32,0},{64,32},{96,64},{128,96},{160,128},{192,160},{224,192},{33,... | collective-permute-start | bytes 1597448 | tf_op jit(solution)/shard_map/ppermute | solution.py:19
  16.9 1.3 %collective-permute-start.1 = (f32[520,256]{1,0:T(8,128)S(1)}, f32[520,256]{1,0:T(8,128)S(1)}, u32[]{:S(2)}, u32[]{:S(2)}) collective-permute-start(f32[520,256]{1,0:T(8,128)S(1)} %get-tuple-element.23), channel_id=1, source_target_pairs={{8,0},{16,8},{24,16},{9,1},{17,9},{25,17},{10,2},{18,10},{26,18},{... | collective-permute-start | bytes 1597448 | tf_op jit(solution)/shard_map/ppermute | solution.py:19
  18.2 0.0 copy-done.4
  18.2 0.1 copy.12
  18.3 0.7 reshape_squeeze.3.picks_ref
  18.9 0.0 collective-permute-done.2.refs_0_
  18.9 0.0 copy-start.1
  18.9 0.8 copy-done.1
  19.7 24.5 %shard_map.95 = (f32[20,8,256]{2,1,0:T(8,128)}, f32[20,8,8]{2,1,0:T(8,128)}) custom-call(f32[1]{0:T(128)} %bitcast.1.scal_ref, s32[160]{0:T(256)} %reshape_squeeze.3.picks_ref, f32[3,4,256,256]{3,2,1,0:T(8,128)} %bitcast.43, f32[520,256]{1,0:T(8,128)} %copy-done.1, f32[2,8,256,256]{3,2,1,0:T(8,128)} %bitcast.45, f32[20,16,256]{2,1,0:T(8,128)} %bitcast.46), custom_call_target="tpu_custom_call" | custom-call | tf_op jit(solution)/shard_map/pallas_call | solution.py:141
  44.2 0.0 copy-start.5
  44.2 0.0 collective-permute-done.refs_0_
  44.2 0.0 copy-start.2
  44.2 9.2 %collective-permute-done.1.refs_1_ = f32[520,256]{1,0:T(8,128)S(1)} collective-permute-done((f32[520,256]{1,0:T(8,128)S(1)}, f32[520,256]{1,0:T(8,128)S(1)}, u32[]{:S(2)}, u32[]{:S(2)}) %collective-permute-start.1) | collective-permute-done | bytes 532512 | tf_op jit(solution)/shard_map/ppermute | solution.py:19
  53.5 0.0 copy-start.3
  53.5 0.0 copy-done.2
  53.5 0.8 copy-done.3
  54.3 19.7 %shard_map.96 = (f32[20,8,256]{2,1,0:T(8,128)}, f32[20,8,8]{2,1,0:T(8,128)}) custom-call(f32[1]{0:T(128)} %bitcast.1.scal_ref, s32[160]{0:T(256)} %reshape_squeeze.3.picks_ref, f32[3,4,256,256]{3,2,1,0:T(8,128)} %bitcast.44, f32[520,256]{1,0:T(8,128)} %copy-done.2, f32[520,256]{1,0:T(8,128)} %copy-done.3, ...), custom_call_target="tpu_custom_call", output_to_operand_aliasing={{0}: (6, {}), {1}: (7, {})} | custom-call | tf_op jit(solution)/shard_map/pallas_call | solution.py:141
  74.0 1.0 %copy.13 = f32[20,8,8]{0,2,1:T(8,128)S(1)} copy(f32[20,8,8]{2,1,0:T(8,128)} %get-tuple-element.9) | data formatting | bytes 10240 | tf_op jit(solution)/shard_map/pallas_call | solution.py:141
  75.0 0.0 copy-done.5
  75.0 0.2 fusion.3
  75.2 0.1 reshape.62
  75.3 10.0 %all_to_all.5 = f32[8,1,1024]{2,1,0:T(1,128)S(1)} all-to-all(f32[8,1,1024]{2,1,0:T(1,128)S(1)} %reshape.62), channel_id=1, replica_groups=mesh['gx'=8,'gy'=4,'gz'=8] {'gz'}, dimensions={0} | all-to-all | bytes 65536 | tf_op jit(solution)/shard_map/all_to_all | solution.py:203
  85.3 0.5 broadcast.35
  85.9 0.7 reduce
  86.6 0.1 reshape.63
  86.7 0.6 reduce_sum.49
  (4 shorter events, 0.1 us)
Async XLA Ops:
  0.7 2.8 %copy-start = (f32[1,1,1,3,4,256,256]{6,5,4,3,2,1,0:T(8,128)S(1)}, f32[1,1,1,3,4,256,256]{6,5,4,3,2,1,0:T(8,128)}, u32[]{:S(2)}) copy-start(f32[1,1,1,3,4,256,256]{6,5,4,3,2,1,0:T(8,128)} %param.9) | copy-start | bytes 9437188
  0.7 3.6 %copy-start.6 = (f32[4]{0:T(128)S(1)}, f32[4]{0:T(128)}, u32[]{:S(2)}) copy-start(f32[4]{0:T(128)} %param.15) | copy-start | bytes 52
  5.7 12.4 %copy-start.4 = (s32[1,1,1,20,8]{3,4,2,1,0:T(8,128)S(1)}, s32[1,1,1,20,8]{3,4,2,1,0:T(8,128)}, u32[]{:S(2)}) copy-start(s32[1,1,1,20,8]{3,4,2,1,0:T(8,128)} %param.12) | copy-start | bytes 1924
  6.2 12.7 %collective-permute-start.2 = (f32[520,256]{1,0:T(8,128)S(1)}, f32[520,256]{1,0:T(8,128)S(1)}, u32[]{:S(2)}, u32[]{:S(2)}) collective-permute-start(f32[520,256]{1,0:T(8,128)S(1)} %get-tuple-element.22), channel_id=1, source_target_pairs={{1,0},{2,1},{3,2},{4,3},{5,4},{6,5},{7,6},{9,8},{10,9},{11,10},{12... | collective-permute-start | bytes 1597448 | tf_op jit(solution)/shard_map/ppermute | solution.py:19
  7.5 36.7 %collective-permute-start = (f32[520,256]{1,0:T(8,128)S(1)}, f32[520,256]{1,0:T(8,128)S(1)}, u32[]{:S(2)}, u32[]{:S(2)}) collective-permute-start(f32[520,256]{1,0:T(8,128)S(1)} %get-tuple-element.24), channel_id=1, source_target_pairs={{32,0},{64,32},{96,64},{128,96},{160,128},{192,160},{224,192},{33,... | collective-permute-start | bytes 1597448 | tf_op jit(solution)/shard_map/ppermute | solution.py:19
  16.9 36.6 %collective-permute-start.1 = (f32[520,256]{1,0:T(8,128)S(1)}, f32[520,256]{1,0:T(8,128)S(1)}, u32[]{:S(2)}, u32[]{:S(2)}) collective-permute-start(f32[520,256]{1,0:T(8,128)S(1)} %get-tuple-element.23), channel_id=1, source_target_pairs={{8,0},{16,8},{24,16},{9,1},{17,9},{25,17},{10,2},{18,10},{26,18},{... | collective-permute-start | bytes 1597448 | tf_op jit(solution)/shard_map/ppermute | solution.py:19
  18.9 0.8 copy-start.1
  44.2 30.7 %copy-start.5 = (s32[1,1,1,20]{3,2,1,0:T(1,128)S(1)}, s32[1,1,1,20]{3,2,1,0:T(1,128)}, u32[]{:S(2)}) copy-start(s32[1,1,1,20]{3,2,1,0:T(1,128)} %param.13) | copy-start | bytes 244
  44.2 9.3 %copy-start.2 = (f32[520,256]{1,0:T(8,128)}, f32[520,256]{1,0:T(8,128)S(1)}, u32[]{:S(2)}) copy-start(f32[520,256]{1,0:T(8,128)S(1)} %collective-permute-done.refs_0_) | copy-start | bytes 1597444
  53.5 0.8 copy-start.3

commit v6 on v4

--- a/solution.py
+++ b/solution.py
@@ -118,6 +118,12 @@
     own = scal_ref[0]
     f = 0
     for a, packed in zip(cross_axes, packed_refs):
+        if len(packed.shape) == 3:
+            for k in range(crossing):
+                m_scr[f] = own * plus_ref[a, k] + packed[k]
+                v_scr[f] = v0_ref[first + f]
+                f += 1
+            continue
         side = packed[pairs * width :, :]
         next_scale = side[pairs : pairs + 1, 0:1]
         for k in range(crossing):
@@ -177,6 +183,9 @@
     packed_in = []
     for a in range(dims):
         halves = minus_local[a]
+        if a == dims - 1:
+            packed_in.append(passed_along(own_scale * halves, axes[a], -1))
+            continue
         packed = jnp.where(col >= row, halves[:pairs], halves[pairs:]).reshape(pairs * width, width)
         diagonals = jnp.sum(jnp.where(col == row, halves[pairs:], 0.0), axis=1)
         scale_row = jnp.broadcast_to(own_scale, (1, width))

time: 89.3 us -> 91.4 us (1.024)
  other arithmetic: 2.61 us -> 6.38 us
  local copies, waits for them, and re-layouts: 7.63 us -> 5.91 us
    mul x0 -> x1, other arithmetic: none -> 1.99 us  [per_device(): packed_in.append(passed_along(own_scale * halves, axes[a], -1))]
    reduce_sum x1, other arithmetic: 0.14 us -> 1.31 us  [per_device(): diagonals = jnp.sum(jnp.where(col == row, halves[pairs:], 0.0), axis=1)]
    unnamed x17 -> x9, local copies, waits for them, and re-layouts: 2.32 us -> 1.26 us
  transfers between devices with their start and end apart: 3 -> 3, of which waited for: 1 -> 1; matrix products, arithmetic and copies ran while one was open for 1% -> 5% of each run, Pallas kernels for 30% -> 30%
where the time goes in v6:
time: 91.4 us; the launch traced here: 91 us
  Pallas kernels  48.5 us (53%)
  starting transfers between devices  11.9 us (13%)
  blocking collectives  10 us (11%)
  waiting for transfers between devices  6.66 us (7%)
  other arithmetic  6.38 us (7%)
  local copies, waits for them, and re-layouts  5.91 us (6%)
  between operations  1.38 us (2%)
    pallas_call x2, Pallas kernels, run_faces(): pl.pallas_call(kernel, out_shape=(jax.ShapeDtypeStruct((total, nsel, widt...  48.5 us
    ppermute x3, starting transfers between devices, passed_along(): return lax.ppermute(block, axis, route)  11.9 us
    all_to_all x1, blocking collectives, per_device(): coarse = jnp.sum(lax.all_to_all(term, 'gz', 0, 0), axis=0)  10 us
    ppermute x3, waiting for transfers between devices, passed_along(): return lax.ppermute(block, axis, route)  6.66 us
    mul x1, other arithmetic, per_device(): packed_in.append(passed_along(own_scale * halves, axes[a], -1))  1.99 us
  transfers between devices with their start and end apart: 3, of which 1 were waited for; matrix products, arithmetic and copies ran while one was open for 5% of the time, Pallas kernels for 30%

profile of v6, /device:TPU:6, one launch (start us, length us, event | category | flops | bytes accessed | tf_op | source)
XLA Modules:
  0.0 91.0 jit_solution(13722590298125249027)
XLA Ops:
  1.3 1.3 %fusion.7 = f32[]{:T(128)} fusion(f32[4]{0:T(128)} %param.15, s32[]{:T(128)} %bitcast.35), kind=kLoop, calls=%fused_computation.18 | loop fusion | flops 11 | bytes 24 | tf_op jit(solution)/shard_map/reduce_sum | solution.py:179
  2.6 2.0 %multiply_bitcast_fusion = f32[4,256,256]{2,1,0:T(8,128)S(1)} fusion(f32[1,1,1,3,4,256,256]{6,5,4,3,2,1,0:T(8,128)} %param.9, f32[]{:T(128)} %fusion.7), kind=kLoop, calls=%fused_computation | loop fusion | flops 262144 | bytes 2097156 | tf_op jit(solution)/shard_map/mul | solution.py:187
  4.6 1.3 %collective-permute-start.2 = (f32[4,256,256]{2,1,0:T(8,128)S(1)}, f32[4,256,256]{2,1,0:T(8,128)S(1)}, u32[]{:S(2)}, u32[]{:S(2)}) collective-permute-start(f32[4,256,256]{2,1,0:T(8,128)S(1)} %multiply_bitcast_fusion), channel_id=1, source_target_pairs={{1,0},{2,1},{3,2},{4,3},{5,4},{6,5},{7,6},{9,8},{10,9},{11,10},{12... | collective-permute-start | bytes 3145736 | tf_op jit(solution)/shard_map/ppermute | solution.py:19
  5.9 1.7 %fusion.8 = (f32[1,1,1,1,2,256,256]{6,5,4,3,2,1,0:T(8,128)S(1)}, f32[1,1,1,1,2,256,256]{6,5,4,3,2,1,0:T(8,128)S(1)}, f32[1,1,1,1,2,256,256]{6,5,4,3,2,1,0:T(8,128)S(1)}, f32[1,1,1,1,2,256,256]{6,5,4,3,2,1,0:T(8,128)S(1)}) fusion(f32[1,1,1,3,4,256,256]{6,5,4,3,2,1,0:T(8,128)} %param.9), kind=kLoop, calls=%fused_computation.19 | loop fusion | bytes 4194304 | tf_op jit(solution)/shard_map/slice | solution.py:189
  7.6 0.8 pad.6.clone
  8.4 0.1 pad.7.clone
  8.4 0.0 copy-start.1
  8.4 0.2 bitcast_select_fusion
  8.6 1.3 %fusion = (f32[2,256]{1,0:T(2,128)S(1)}, f32[2,256]{1,0:T(2,128)S(1)}) fusion(pred[256,256]{1,0:T(8,128)(4,1)S(1)} %iota_compare_fusion, f32[1,1,1,3,4,256,256]{6,5,4,3,2,1,0:T(8,128)} %param.9), kind=kLoop, calls=%fused_computation.6 | loop fusion | flops 523264 | bytes 1118208 | tf_op jit(solution)/shard_map/reduce_sum | solution.py:190
  9.9 0.2 maximum_maximum_fusion.1
  10.1 9.4 %collective-permute-start = (f32[520,256]{1,0:T(8,128)S(1)}, f32[520,256]{1,0:T(8,128)}, u32[]{:S(2)}, u32[]{:S(2)}) collective-permute-start(f32[520,256]{1,0:T(8,128)S(1)} %get-tuple-element.19), channel_id=1, source_target_pairs={{32,0},{64,32},{96,64},{128,96},{160,128},{192,160},{224,192},{33,... | collective-permute-start | bytes 1597448 | tf_op jit(solution)/shard_map/ppermute | solution.py:19
  19.5 1.3 %collective-permute-start.1 = (f32[520,256]{1,0:T(8,128)S(1)}, f32[520,256]{1,0:T(8,128)}, u32[]{:S(2)}, u32[]{:S(2)}) collective-permute-start(f32[520,256]{1,0:T(8,128)S(1)} %get-tuple-element.18), channel_id=1, source_target_pairs={{8,0},{16,8},{24,16},{9,1},{17,9},{25,17},{10,2},{18,10},{26,18},{... | collective-permute-start | bytes 1597448 | tf_op jit(solution)/shard_map/ppermute | solution.py:19
  20.8 0.0 copy-done.1
  20.8 0.1 copy.12
  20.9 0.7 reshape_squeeze.3.picks_ref
  21.6 0.0 collective-permute-done.2.refs_0_
  21.6 0.0 copy-start
  21.6 1.0 %copy-done = f32[4,256,256]{2,1,0:T(8,128)} copy-done((f32[4,256,256]{2,1,0:T(8,128)}, f32[4,256,256]{2,1,0:T(8,128)S(1)}, u32[]{:S(2)}) %copy-start) | copy-done | bytes 1048600
  22.6 27.0 %shard_map.95 = (f32[20,8,256]{2,1,0:T(8,128)}, f32[20,8,8]{2,1,0:T(8,128)}) custom-call(f32[1]{0:T(128)} %bitcast.1.scal_ref, s32[160]{0:T(256)} %reshape_squeeze.3.picks_ref, f32[3,4,256,256]{3,2,1,0:T(8,128)} %bitcast.36, f32[4,256,256]{2,1,0:T(8,128)} %copy-done, f32[2,8,256,256]{3,2,1,0:T(8,128)} %bitcast.38, f32[20,16,256]{2,1,0:T(8,128)} %bitcast.39), custom_call_target="tpu_custom_call" | custom-call | tf_op jit(solution)/shard_map/pallas_call | solution.py:147
  49.6 0.0 copy-start.2
  49.6 0.0 collective-permute-done.refs_0_
  49.6 6.7 %collective-permute-done.1.refs_1_ = f32[520,256]{1,0:T(8,128)} collective-permute-done((f32[520,256]{1,0:T(8,128)S(1)}, f32[520,256]{1,0:T(8,128)}, u32[]{:S(2)}, u32[]{:S(2)}) %collective-permute-start.1) | collective-permute-done | bytes 532512 | tf_op jit(solution)/shard_map/ppermute | solution.py:19
  56.2 21.5 %shard_map.96 = (f32[20,8,256]{2,1,0:T(8,128)}, f32[20,8,8]{2,1,0:T(8,128)}) custom-call(f32[1]{0:T(128)} %bitcast.1.scal_ref, s32[160]{0:T(256)} %reshape_squeeze.3.picks_ref, f32[3,4,256,256]{3,2,1,0:T(8,128)} %bitcast.37, f32[520,256]{1,0:T(8,128)} %collective-permute-done.refs_0_, ...), custom_call_target="tpu_custom_call", output_to_operand_aliasing={{0}: (6, {}), {1}: (7, {})} | custom-call | tf_op jit(solution)/shard_map/pallas_call | solution.py:147
  77.7 1.0 %copy.13 = f32[20,8,8]{0,2,1:T(8,128)S(1)} copy(f32[20,8,8]{2,1,0:T(8,128)} %get-tuple-element.9) | data formatting | bytes 10240 | tf_op jit(solution)/shard_map/pallas_call | solution.py:147
  78.7 0.0 copy-done.2
  78.7 0.2 fusion.2
  78.9 0.1 reshape.58
  79.0 10.0 %all_to_all.5 = f32[8,1,1024]{2,1,0:T(1,128)S(1)} all-to-all(f32[8,1,1024]{2,1,0:T(1,128)S(1)} %reshape.58), channel_id=1, replica_groups=mesh['gx'=8,'gy'=4,'gz'=8] {'gz'}, dimensions={0} | all-to-all | bytes 65536 | tf_op jit(solution)/shard_map/all_to_all | solution.py:212
  89.1 0.5 broadcast.34
  89.6 0.7 reduce
  90.3 0.1 reshape.59
  90.4 0.6 reduce_sum.39
  (4 shorter events, 0.1 us)
Async XLA Ops:
  4.6 17.0 %collective-permute-start.2 = (f32[4,256,256]{2,1,0:T(8,128)S(1)}, f32[4,256,256]{2,1,0:T(8,128)S(1)}, u32[]{:S(2)}, u32[]{:S(2)}) collective-permute-start(f32[4,256,256]{2,1,0:T(8,128)S(1)} %multiply_bitcast_fusion), channel_id=1, source_target_pairs={{1,0},{2,1},{3,2},{4,3},{5,4},{6,5},{7,6},{9,8},{10,9},{11,10},{12... | collective-permute-start | bytes 3145736 | tf_op jit(solution)/shard_map/ppermute | solution.py:19
  8.4 12.4 %copy-start.1 = (s32[1,1,1,20,8]{3,4,2,1,0:T(8,128)S(1)}, s32[1,1,1,20,8]{3,4,2,1,0:T(8,128)}, u32[]{:S(2)}) copy-start(s32[1,1,1,20,8]{3,4,2,1,0:T(8,128)} %param.12) | copy-start | bytes 1924
  10.1 39.4 %collective-permute-start = (f32[520,256]{1,0:T(8,128)S(1)}, f32[520,256]{1,0:T(8,128)}, u32[]{:S(2)}, u32[]{:S(2)}) collective-permute-start(f32[520,256]{1,0:T(8,128)S(1)} %get-tuple-element.19), channel_id=1, source_target_pairs={{32,0},{64,32},{96,64},{128,96},{160,128},{192,160},{224,192},{33,... | collective-permute-start | bytes 1597448 | tf_op jit(solution)/shard_map/ppermute | solution.py:19
  19.5 36.7 %collective-permute-start.1 = (f32[520,256]{1,0:T(8,128)S(1)}, f32[520,256]{1,0:T(8,128)}, u32[]{:S(2)}, u32[]{:S(2)}) collective-permute-start(f32[520,256]{1,0:T(8,128)S(1)} %get-tuple-element.18), channel_id=1, source_target_pairs={{8,0},{16,8},{24,16},{9,1},{17,9},{25,17},{10,2},{18,10},{26,18},{... | collective-permute-start | bytes 1597448 | tf_op jit(solution)/shard_map/ppermute | solution.py:19
  21.6 1.0 %copy-start = (f32[4,256,256]{2,1,0:T(8,128)}, f32[4,256,256]{2,1,0:T(8,128)S(1)}, u32[]{:S(2)}) copy-start(f32[4,256,256]{2,1,0:T(8,128)S(1)} %collective-permute-done.2.refs_0_) | copy-start | bytes 3145732
  49.6 29.1 %copy-start.2 = (s32[1,1,1,20]{3,2,1,0:T(1,128)S(1)}, s32[1,1,1,20]{3,2,1,0:T(1,128)}, u32[]{:S(2)}) copy-start(s32[1,1,1,20]{3,2,1,0:T(1,128)} %param.13) | copy-start | bytes 244

commit v7 on v4

--- a/solution.py
+++ b/solution.py
@@ -121,7 +121,7 @@
         side = packed[pairs * width :, :]
         next_scale = side[pairs : pairs + 1, 0:1]
         for k in range(crossing):
-            m_scr[f] = own * plus_ref[a, k] + next_scale * unpacked(packed, side, k, pairs)
+            m_scr[f] = own * plus_ref[a - cross_axes[0], k] + next_scale * unpacked(packed, side, k, pairs)
             v_scr[f] = v0_ref[first + f]
             f += 1
     if with_inner:
@@ -132,20 +132,27 @@
     iterate(own, picks_ref, first, c_ref, e_ref, m_scr, v_scr, w_scr)
 
 
-def run_faces(kernel, faces, nsel, width, count, smem_args, vmem_args, earlier=()):
+def run_faces(kernel, faces, nsel, width, count, smem_args, vmem_args, axes, earlier=()):
     vmem = pltpu.MemorySpace.VMEM
     smem = pltpu.MemorySpace.SMEM
     total = vmem_args[-1].shape[0]
     args = (*smem_args, *vmem_args, *earlier)
     aliases = {len(args) - len(earlier) + i: i for i in range(len(earlier))}
+    plus_shape = vmem_args[0].shape
+    lowest = axes[0]
+    plus_spec = pl.BlockSpec(
+        (len(axes),) + plus_shape[1:], lambda i: (lowest // len(axes), 0, 0, 0), memory_space=vmem
+    )
     return pl.pallas_call(
         kernel,
+        grid=(1,),
         out_shape=(
             jax.ShapeDtypeStruct((total, nsel, width), jnp.float32),
             jax.ShapeDtypeStruct((total, nsel, nsel), jnp.float32),
         ),
         in_specs=[pl.BlockSpec(memory_space=smem)] * len(smem_args)
-        + [pl.BlockSpec(memory_space=vmem)] * (len(vmem_args) + len(earlier)),
+        + [plus_spec]
+        + [pl.BlockSpec(memory_space=vmem)] * (len(vmem_args) - 1 + len(earlier)),
         out_specs=(pl.BlockSpec(memory_space=vmem), pl.BlockSpec(memory_space=vmem)),
         scratch_shapes=[
             pltpu.VMEM((faces, width, width), jnp.float32),
@@ -189,11 +196,11 @@
     late = tuple(range(dims - 1))
     early_c, early_e = run_faces(
         functools.partial(face_kernel, (dims - 1,), True), crossing + n_inner, nsel, width, count,
-        (scal, picks_flat), (plus_local, packed_in[dims - 1], inner_local, basis_vectors),
+        (scal, picks_flat), (plus_local, packed_in[dims - 1], inner_local, basis_vectors), (dims - 1,),
     )
     constraints, blocks = run_faces(
         functools.partial(face_kernel, late, False), len(late) * crossing, nsel, width, count,
-        (scal, picks_flat), (plus_local, *packed_in[: dims - 1], basis_vectors), (early_c, early_e),
+        (scal, picks_flat), (plus_local, *packed_in[: dims - 1], basis_vectors), late, (early_c, early_e),
     )
     flat = blocks.reshape(faces_all, -1)
     groups = lax.axis_size("gz")

time: 89.3 us -> 89 us (level)
  Pallas kernels: 48.5 us -> 47.6 us
    pallas_call x2, Pallas kernels: 48.5 us -> 47.6 us  [run_faces(): pl.pallas_call(kernel, grid=(1,), out_shape=(jax.ShapeDtypeStruct((total,...]
where the time goes in v7:
time: 89 us; the launch traced here: 88.7 us
  Pallas kernels  47.6 us (53%)
  starting transfers between devices  11.9 us (13%)
  blocking collectives  10 us (11%)
  local copies, waits for them, and re-layouts  7.63 us (9%)
  waiting for transfers between devices  7.29 us (8%)
  other arithmetic  2.61 us (3%)
  between operations  1.41 us (2%)
    pallas_call x2, Pallas kernels, run_faces(): pl.pallas_call(kernel, grid=(1,), out_shape=(jax.ShapeDtypeStruct((total,...  47.6 us
    ppermute x3, starting transfers between devices, passed_along(): return lax.ppermute(block, axis, route)  11.9 us
    all_to_all x1, blocking collectives, per_device(): coarse = jnp.sum(lax.all_to_all(term, 'gz', 0, 0), axis=0)  10 us
    ppermute x3, waiting for transfers between devices, passed_along(): return lax.ppermute(block, axis, route)  7.29 us
    slice x1, local copies, waits for them, and re-layouts, per_device(): halves[:pairs]  2.36 us
    unnamed x17, local copies, waits for them, and re-layouts  2.32 us
  transfers between devices with their start and end apart: 3, of which 1 were waited for; matrix products, arithmetic and copies ran while one was open for 1% of the time, Pallas kernels for 30%

profile of v7, /device:TPU:6, one launch (start us, length us, event | category | flops | bytes accessed | tf_op | source)
XLA Modules:
  0.0 88.7 jit_solution(15814414683769212768)
XLA Ops:
  0.7 0.0 copy-start
  0.7 0.0 copy-start.6
  0.7 2.4 %fusion.9 = (f32[1,1,1,1,2,256,256]{6,5,4,3,2,1,0:T(8,128)S(1)}, f32[1,1,1,1,2,256,256]{6,5,4,3,2,1,0:T(8,128)S(1)}, f32[1,1,1,1,2,256,256]{6,5,4,3,2,1,0:T(8,12...) fusion(f32[1,1,1,3,4,256,256]{6,5,4,3,2,1,0:T(8,128)} %param.9), kind=kLoop, calls=%fused_computation.22 | loop fusion | bytes 6291456 | tf_op jit(solution)/shard_map/slice | solution.py:187
  3.1 0.4 copy-done
  3.5 0.1 fusion
  4.3 0.0 copy-done.6
  4.3 0.6 fusion.8
  5.0 0.7 pad.10.clone
  5.7 0.1 pad.11.clone
  5.7 0.0 copy-start.4
  5.8 0.2 bitcast_select_fusion
  6.0 0.2 maximum_maximum_fusion.2
  6.2 1.3 %collective-permute-start.2 = (f32[520,256]{1,0:T(8,128)S(1)}, f32[520,256]{1,0:T(8,128)S(1)}, u32[]{:S(2)}, u32[]{:S(2)}) collective-permute-start(f32[520,256]{1,0:T(8,128)S(1)} %get-tuple-element.22), channel_id=1, source_target_pairs={{1,0},{2,1},{3,2},{4,3},{5,4},{6,5},{7,6},{9,8},{10,9},{11,10},{12... | collective-permute-start | bytes 1597448 | tf_op jit(solution)/shard_map/ppermute | solution.py:19
  7.5 9.4 %collective-permute-start = (f32[520,256]{1,0:T(8,128)S(1)}, f32[520,256]{1,0:T(8,128)S(1)}, u32[]{:S(2)}, u32[]{:S(2)}) collective-permute-start(f32[520,256]{1,0:T(8,128)S(1)} %get-tuple-element.24), channel_id=1, source_target_pairs={{32,0},{64,32},{96,64},{128,96},{160,128},{192,160},{224,192},{33,... | collective-permute-start | bytes 1597448 | tf_op jit(solution)/shard_map/ppermute | solution.py:19
  16.9 1.3 %collective-permute-start.1 = (f32[520,256]{1,0:T(8,128)S(1)}, f32[520,256]{1,0:T(8,128)S(1)}, u32[]{:S(2)}, u32[]{:S(2)}) collective-permute-start(f32[520,256]{1,0:T(8,128)S(1)} %get-tuple-element.23), channel_id=1, source_target_pairs={{8,0},{16,8},{24,16},{9,1},{17,9},{25,17},{10,2},{18,10},{26,18},{... | collective-permute-start | bytes 1597448 | tf_op jit(solution)/shard_map/ppermute | solution.py:19
  18.2 0.0 copy-done.4
  18.2 0.1 copy.12
  18.3 0.7 reshape_squeeze.3.picks_ref
  18.9 0.0 collective-permute-done.2.refs_0_
  18.9 0.0 copy-start.1
  18.9 0.8 copy-done.1
  19.7 26.5 %shard_map.95 = (f32[20,8,256]{2,1,0:T(8,128)}, f32[20,8,8]{2,1,0:T(8,128)}) custom-call(f32[1]{0:T(128)} %bitcast.1.scal_ref, s32[160]{0:T(256)} %reshape_squeeze.3.picks_ref, f32[3,4,256,256]{3,2,1,0:T(8,128)} %bitcast.43, f32[520,256]{1,0:T(8,128)} %copy-done.1, f32[2,8,256,256]{3,2,1,0:T(8,128)} %bitcast.45, f32[20,16,256]{2,1,0:T(8,128)} %bitcast.46), custom_call_target="tpu_custom_call" | custom-call | tf_op jit(solution)/shard_map/pallas_call | solution.py:146
  46.2 0.0 copy-start.5
  46.2 0.0 collective-permute-done.refs_0_
  46.2 0.0 copy-start.2
  46.2 7.3 %collective-permute-done.1.refs_1_ = f32[520,256]{1,0:T(8,128)S(1)} collective-permute-done((f32[520,256]{1,0:T(8,128)S(1)}, f32[520,256]{1,0:T(8,128)S(1)}, u32[]{:S(2)}, u32[]{:S(2)}) %collective-permute-start.1) | collective-permute-done | bytes 532512 | tf_op jit(solution)/shard_map/ppermute | solution.py:19
  53.5 0.0 copy-start.3
  53.5 0.0 copy-done.2
  53.5 0.8 copy-done.3
  54.3 21.1 %shard_map.96 = (f32[20,8,256]{2,1,0:T(8,128)}, f32[20,8,8]{2,1,0:T(8,128)}) custom-call(f32[1]{0:T(128)} %bitcast.1.scal_ref, s32[160]{0:T(256)} %reshape_squeeze.3.picks_ref, f32[3,4,256,256]{3,2,1,0:T(8,128)} %bitcast.44, f32[520,256]{1,0:T(8,128)} %copy-done.2, f32[520,256]{1,0:T(8,128)} %copy-done.3, ...), custom_call_target="tpu_custom_call", output_to_operand_aliasing={{0}: (6, {}), {1}: (7, {})} | custom-call | tf_op jit(solution)/shard_map/pallas_call | solution.py:146
  75.4 1.0 %copy.13 = f32[20,8,8]{0,2,1:T(8,128)S(1)} copy(f32[20,8,8]{2,1,0:T(8,128)} %get-tuple-element.9) | data formatting | bytes 10240 | tf_op jit(solution)/shard_map/pallas_call | solution.py:146
  76.4 0.0 copy-done.5
  76.4 0.2 fusion.3
  76.6 0.1 reshape.62
  76.7 10.0 %all_to_all.5 = f32[8,1,1024]{2,1,0:T(1,128)S(1)} all-to-all(f32[8,1,1024]{2,1,0:T(1,128)S(1)} %reshape.62), channel_id=1, replica_groups=mesh['gx'=8,'gy'=4,'gz'=8] {'gz'}, dimensions={0} | all-to-all | bytes 65536 | tf_op jit(solution)/shard_map/all_to_all | solution.py:210
  86.8 0.5 broadcast.35
  87.3 0.7 reduce
  88.0 0.1 reshape.63
  88.1 0.6 reduce_sum.49
  (4 shorter events, 0.1 us)
Async XLA Ops:
  0.7 2.8 %copy-start = (f32[1,1,1,3,4,256,256]{6,5,4,3,2,1,0:T(8,128)S(1)}, f32[1,1,1,3,4,256,256]{6,5,4,3,2,1,0:T(8,128)}, u32[]{:S(2)}) copy-start(f32[1,1,1,3,4,256,256]{6,5,4,3,2,1,0:T(8,128)} %param.9) | copy-start | bytes 9437188
  0.7 3.6 %copy-start.6 = (f32[4]{0:T(128)S(1)}, f32[4]{0:T(128)}, u32[]{:S(2)}) copy-start(f32[4]{0:T(128)} %param.15) | copy-start | bytes 52
  5.7 12.4 %copy-start.4 = (s32[1,1,1,20,8]{3,4,2,1,0:T(8,128)S(1)}, s32[1,1,1,20,8]{3,4,2,1,0:T(8,128)}, u32[]{:S(2)}) copy-start(s32[1,1,1,20,8]{3,4,2,1,0:T(8,128)} %param.12) | copy-start | bytes 1924
  6.2 12.7 %collective-permute-start.2 = (f32[520,256]{1,0:T(8,128)S(1)}, f32[520,256]{1,0:T(8,128)S(1)}, u32[]{:S(2)}, u32[]{:S(2)}) collective-permute-start(f32[520,256]{1,0:T(8,128)S(1)} %get-tuple-element.22), channel_id=1, source_target_pairs={{1,0},{2,1},{3,2},{4,3},{5,4},{6,5},{7,6},{9,8},{10,9},{11,10},{12... | collective-permute-start | bytes 1597448 | tf_op jit(solution)/shard_map/ppermute | solution.py:19
  7.5 38.7 %collective-permute-start = (f32[520,256]{1,0:T(8,128)S(1)}, f32[520,256]{1,0:T(8,128)S(1)}, u32[]{:S(2)}, u32[]{:S(2)}) collective-permute-start(f32[520,256]{1,0:T(8,128)S(1)} %get-tuple-element.24), channel_id=1, source_target_pairs={{32,0},{64,32},{96,64},{128,96},{160,128},{192,160},{224,192},{33,... | collective-permute-start | bytes 1597448 | tf_op jit(solution)/shard_map/ppermute | solution.py:19
  16.9 36.6 %collective-permute-start.1 = (f32[520,256]{1,0:T(8,128)S(1)}, f32[520,256]{1,0:T(8,128)S(1)}, u32[]{:S(2)}, u32[]{:S(2)}) collective-permute-start(f32[520,256]{1,0:T(8,128)S(1)} %get-tuple-element.23), channel_id=1, source_target_pairs={{8,0},{16,8},{24,16},{9,1},{17,9},{25,17},{10,2},{18,10},{26,18},{... | collective-permute-start | bytes 1597448 | tf_op jit(solution)/shard_map/ppermute | solution.py:19
  18.9 0.8 copy-start.1
  46.2 30.2 %copy-start.5 = (s32[1,1,1,20]{3,2,1,0:T(1,128)S(1)}, s32[1,1,1,20]{3,2,1,0:T(1,128)}, u32[]{:S(2)}) copy-start(s32[1,1,1,20]{3,2,1,0:T(1,128)} %param.13) | copy-start | bytes 244
  46.2 7.3 %copy-start.2 = (f32[520,256]{1,0:T(8,128)}, f32[520,256]{1,0:T(8,128)S(1)}, u32[]{:S(2)}) copy-start(f32[520,256]{1,0:T(8,128)S(1)} %collective-permute-done.refs_0_) | copy-start | bytes 1597444
  53.5 0.8 copy-start.3

commit v8 on v7

--- a/solution.py
+++ b/solution.py
@@ -62,7 +62,7 @@
         return carry
 
     for iteration in range(ITERS):
-        lax.fori_loop(0, faces, image, 0, unroll=4)
+        lax.fori_loop(0, faces, image, 0, unroll=8)
         images = [w_scr[g0:g1].reshape((g1 - g0) * count, -1) for g0, g1 in spans]
         grams = [
             lax.dot_general(

time: 89 us -> 87.8 us (0.987)
  transfers between devices with their start and end apart: 3 -> 3, of which waited for: 1 -> 1; matrix products, arithmetic and copies ran while one was open for 1% -> 1% of each run, Pallas kernels for 30% -> 31%
where the time goes in v8:
time: 87.8 us; the launch traced here: 87.5 us
  Pallas kernels  46.8 us (53%)
  starting transfers between devices  11.9 us (14%)
  blocking collectives  10 us (11%)
  local copies, waits for them, and re-layouts  7.63 us (9%)
  waiting for transfers between devices  6.81 us (8%)
  other arithmetic  2.61 us (3%)
  between operations  1.41 us (2%)
    pallas_call x2, Pallas kernels, run_faces(): pl.pallas_call(kernel, grid=(1,), out_shape=(jax.ShapeDtypeStruct((total,...  46.8 us
    ppermute x3, starting transfers between devices, passed_along(): return lax.ppermute(block, axis, route)  11.9 us
    all_to_all x1, blocking collectives, per_device(): coarse = jnp.sum(lax.all_to_all(term, 'gz', 0, 0), axis=0)  10 us
    ppermute x3, waiting for transfers between devices, passed_along(): return lax.ppermute(block, axis, route)  6.81 us
    slice x1, local copies, waits for them, and re-layouts, per_device(): halves[:pairs]  2.36 us
    unnamed x17, local copies, waits for them, and re-layouts  2.32 us
  transfers between devices with their start and end apart: 3, of which 1 were waited for; matrix products, arithmetic and copies ran while one was open for 1% of the time, Pallas kernels for 31%

profile of v8, /device:TPU:6, one launch (start us, length us, event | category | flops | bytes accessed | tf_op | source)
XLA Modules:
  0.0 87.5 jit_solution(9188628681899854397)
XLA Ops:
  0.7 0.0 copy-start
  0.7 0.0 copy-start.6
  0.7 2.4 %fusion.9 = (f32[1,1,1,1,2,256,256]{6,5,4,3,2,1,0:T(8,128)S(1)}, f32[1,1,1,1,2,256,256]{6,5,4,3,2,1,0:T(8,128)S(1)}, f32[1,1,1,1,2,256,256]{6,5,4,3,2,1,0:T(8,12...) fusion(f32[1,1,1,3,4,256,256]{6,5,4,3,2,1,0:T(8,128)} %param.9), kind=kLoop, calls=%fused_computation.22 | loop fusion | bytes 6291456 | tf_op jit(solution)/shard_map/slice | solution.py:187
  3.1 0.4 copy-done
  3.5 0.1 fusion
  4.3 0.0 copy-done.6
  4.3 0.6 fusion.8
  5.0 0.7 pad.10.clone
  5.7 0.1 pad.11.clone
  5.7 0.0 copy-start.4
  5.8 0.2 bitcast_select_fusion
  6.0 0.2 maximum_maximum_fusion.2
  6.2 1.3 %collective-permute-start.2 = (f32[520,256]{1,0:T(8,128)S(1)}, f32[520,256]{1,0:T(8,128)S(1)}, u32[]{:S(2)}, u32[]{:S(2)}) collective-permute-start(f32[520,256]{1,0:T(8,128)S(1)} %get-tuple-element.22), channel_id=1, source_target_pairs={{1,0},{2,1},{3,2},{4,3},{5,4},{6,5},{7,6},{9,8},{10,9},{11,10},{12... | collective-permute-start | bytes 1597448 | tf_op jit(solution)/shard_map/ppermute | solution.py:19
  7.5 9.4 %collective-permute-start = (f32[520,256]{1,0:T(8,128)S(1)}, f32[520,256]{1,0:T(8,128)S(1)}, u32[]{:S(2)}, u32[]{:S(2)}) collective-permute-start(f32[520,256]{1,0:T(8,128)S(1)} %get-tuple-element.24), channel_id=1, source_target_pairs={{32,0},{64,32},{96,64},{128,96},{160,128},{192,160},{224,192},{33,... | collective-permute-start | bytes 1597448 | tf_op jit(solution)/shard_map/ppermute | solution.py:19
  16.9 1.3 %collective-permute-start.1 = (f32[520,256]{1,0:T(8,128)S(1)}, f32[520,256]{1,0:T(8,128)S(1)}, u32[]{:S(2)}, u32[]{:S(2)}) collective-permute-start(f32[520,256]{1,0:T(8,128)S(1)} %get-tuple-element.23), channel_id=1, source_target_pairs={{8,0},{16,8},{24,16},{9,1},{17,9},{25,17},{10,2},{18,10},{26,18},{... | collective-permute-start | bytes 1597448 | tf_op jit(solution)/shard_map/ppermute | solution.py:19
  18.2 0.0 copy-done.4
  18.2 0.1 copy.12
  18.3 0.7 reshape_squeeze.3.picks_ref
  18.9 0.0 collective-permute-done.2.refs_0_
  18.9 0.0 copy-start.1
  18.9 0.8 copy-done.1
  19.7 26.9 %shard_map.95 = (f32[20,8,256]{2,1,0:T(8,128)}, f32[20,8,8]{2,1,0:T(8,128)}) custom-call(f32[1]{0:T(128)} %bitcast.1.scal_ref, s32[160]{0:T(256)} %reshape_squeeze.3.picks_ref, f32[3,4,256,256]{3,2,1,0:T(8,128)} %bitcast.43, f32[520,256]{1,0:T(8,128)} %copy-done.1, f32[2,8,256,256]{3,2,1,0:T(8,128)} %bitcast.45, f32[20,16,256]{2,1,0:T(8,128)} %bitcast.46), custom_call_target="tpu_custom_call" | custom-call | tf_op jit(solution)/shard_map/pallas_call | solution.py:146
  46.7 0.0 copy-start.5
  46.7 0.0 collective-permute-done.refs_0_
  46.7 0.0 copy-start.2
  46.7 6.8 %collective-permute-done.1.refs_1_ = f32[520,256]{1,0:T(8,128)S(1)} collective-permute-done((f32[520,256]{1,0:T(8,128)S(1)}, f32[520,256]{1,0:T(8,128)S(1)}, u32[]{:S(2)}, u32[]{:S(2)}) %collective-permute-start.1) | collective-permute-done | bytes 532512 | tf_op jit(solution)/shard_map/ppermute | solution.py:19
  53.5 0.0 copy-start.3
  53.5 0.0 copy-done.2
  53.5 0.8 copy-done.3
  54.3 19.8 %shard_map.96 = (f32[20,8,256]{2,1,0:T(8,128)}, f32[20,8,8]{2,1,0:T(8,128)}) custom-call(f32[1]{0:T(128)} %bitcast.1.scal_ref, s32[160]{0:T(256)} %reshape_squeeze.3.picks_ref, f32[3,4,256,256]{3,2,1,0:T(8,128)} %bitcast.44, f32[520,256]{1,0:T(8,128)} %copy-done.2, f32[520,256]{1,0:T(8,128)} %copy-done.3, ...), custom_call_target="tpu_custom_call", output_to_operand_aliasing={{0}: (6, {}), {1}: (7, {})} | custom-call | tf_op jit(solution)/shard_map/pallas_call | solution.py:146
  74.2 1.0 %copy.13 = f32[20,8,8]{0,2,1:T(8,128)S(1)} copy(f32[20,8,8]{2,1,0:T(8,128)} %get-tuple-element.9) | data formatting | bytes 10240 | tf_op jit(solution)/shard_map/pallas_call | solution.py:146
  75.2 0.0 copy-done.5
  75.2 0.2 fusion.3
  75.4 0.1 reshape.62
  75.5 10.0 %all_to_all.5 = f32[8,1,1024]{2,1,0:T(1,128)S(1)} all-to-all(f32[8,1,1024]{2,1,0:T(1,128)S(1)} %reshape.62), channel_id=1, replica_groups=mesh['gx'=8,'gy'=4,'gz'=8] {'gz'}, dimensions={0} | all-to-all | bytes 65536 | tf_op jit(solution)/shard_map/all_to_all | solution.py:210
  85.5 0.5 broadcast.35
  86.0 0.7 reduce
  86.8 0.1 reshape.63
  86.8 0.6 reduce_sum.49
  (4 shorter events, 0.1 us)
Async XLA Ops:
  0.7 2.8 %copy-start = (f32[1,1,1,3,4,256,256]{6,5,4,3,2,1,0:T(8,128)S(1)}, f32[1,1,1,3,4,256,256]{6,5,4,3,2,1,0:T(8,128)}, u32[]{:S(2)}) copy-start(f32[1,1,1,3,4,256,256]{6,5,4,3,2,1,0:T(8,128)} %param.9) | copy-start | bytes 9437188
  0.7 3.6 %copy-start.6 = (f32[4]{0:T(128)S(1)}, f32[4]{0:T(128)}, u32[]{:S(2)}) copy-start(f32[4]{0:T(128)} %param.15) | copy-start | bytes 52
  5.7 12.4 %copy-start.4 = (s32[1,1,1,20,8]{3,4,2,1,0:T(8,128)S(1)}, s32[1,1,1,20,8]{3,4,2,1,0:T(8,128)}, u32[]{:S(2)}) copy-start(s32[1,1,1,20,8]{3,4,2,1,0:T(8,128)} %param.12) | copy-start | bytes 1924
  6.2 12.7 %collective-permute-start.2 = (f32[520,256]{1,0:T(8,128)S(1)}, f32[520,256]{1,0:T(8,128)S(1)}, u32[]{:S(2)}, u32[]{:S(2)}) collective-permute-start(f32[520,256]{1,0:T(8,128)S(1)} %get-tuple-element.22), channel_id=1, source_target_pairs={{1,0},{2,1},{3,2},{4,3},{5,4},{6,5},{7,6},{9,8},{10,9},{11,10},{12... | collective-permute-start | bytes 1597448 | tf_op jit(solution)/shard_map/ppermute | solution.py:19
  7.5 39.2 %collective-permute-start = (f32[520,256]{1,0:T(8,128)S(1)}, f32[520,256]{1,0:T(8,128)S(1)}, u32[]{:S(2)}, u32[]{:S(2)}) collective-permute-start(f32[520,256]{1,0:T(8,128)S(1)} %get-tuple-element.24), channel_id=1, source_target_pairs={{32,0},{64,32},{96,64},{128,96},{160,128},{192,160},{224,192},{33,... | collective-permute-start | bytes 1597448 | tf_op jit(solution)/shard_map/ppermute | solution.py:19
  16.9 36.6 %collective-permute-start.1 = (f32[520,256]{1,0:T(8,128)S(1)}, f32[520,256]{1,0:T(8,128)S(1)}, u32[]{:S(2)}, u32[]{:S(2)}) collective-permute-start(f32[520,256]{1,0:T(8,128)S(1)} %get-tuple-element.23), channel_id=1, source_target_pairs={{8,0},{16,8},{24,16},{9,1},{17,9},{25,17},{10,2},{18,10},{26,18},{... | collective-permute-start | bytes 1597448 | tf_op jit(solution)/shard_map/ppermute | solution.py:19
  18.9 0.8 copy-start.1
  46.7 28.5 %copy-start.5 = (s32[1,1,1,20]{3,2,1,0:T(1,128)S(1)}, s32[1,1,1,20]{3,2,1,0:T(1,128)}, u32[]{:S(2)}) copy-start(s32[1,1,1,20]{3,2,1,0:T(1,128)} %param.13) | copy-start | bytes 244
  46.7 6.8 %copy-start.2 = (f32[520,256]{1,0:T(8,128)}, f32[520,256]{1,0:T(8,128)S(1)}, u32[]{:S(2)}) copy-start(f32[520,256]{1,0:T(8,128)S(1)} %collective-permute-done.refs_0_) | copy-start | bytes 1597444
  53.5 0.8 copy-start.3

commit v9 on v8

--- a/solution.py
+++ b/solution.py
@@ -86,7 +86,7 @@
         e_ref[first + f] = block / own
         return carry
 
-    lax.fori_loop(0, faces, finish, 0, unroll=2)
+    lax.fori_loop(0, faces, finish, 0, unroll=8)
 
 
 def unpacked(packed, side, index, pairs):

time: 87.8 us -> 87 us (level)
  Pallas kernels: 46.8 us -> 45.4 us
    pallas_call x2, Pallas kernels: 46.8 us -> 45.4 us  [run_faces(): pl.pallas_call(kernel, grid=(1,), out_shape=(jax.ShapeDtypeStruct((total,...]
  transfers between devices with their start and end apart: 3 -> 3, of which waited for: 1 -> 1; matrix products, arithmetic and copies ran while one was open for 1% -> 1% of each run, Pallas kernels for 31% -> 30%
where the time goes in v9:
time: 87 us; the launch traced here: 86.7 us
  Pallas kernels  45.4 us (52%)
  starting transfers between devices  11.9 us (14%)
  blocking collectives  10 us (11%)
  local copies, waits for them, and re-layouts  7.63 us (9%)
  waiting for transfers between devices  7.45 us (9%)
  other arithmetic  2.61 us (3%)
  between operations  1.41 us (2%)
    pallas_call x2, Pallas kernels, run_faces(): pl.pallas_call(kernel, grid=(1,), out_shape=(jax.ShapeDtypeStruct((total,...  45.4 us
    ppermute x3, starting transfers between devices, passed_along(): return lax.ppermute(block, axis, route)  11.9 us
    all_to_all x1, blocking collectives, per_device(): coarse = jnp.sum(lax.all_to_all(term, 'gz', 0, 0), axis=0)  10 us
    ppermute x3, waiting for transfers between devices, passed_along(): return lax.ppermute(block, axis, route)  7.45 us
    slice x1, local copies, waits for them, and re-layouts, per_device(): halves[:pairs]  2.36 us
    unnamed x17, local copies, waits for them, and re-layouts  2.32 us
  transfers between devices with their start and end apart: 3, of which 1 were waited for; matrix products, arithmetic and copies ran while one was open for 1% of the time, Pallas kernels for 30%

profile of v9, /device:TPU:6, one launch (start us, length us, event | category | flops | bytes accessed | tf_op | source)
XLA Modules:
  0.0 86.7 jit_solution(14906966142164918467)
XLA Ops:
  0.7 0.0 copy-start
  0.7 0.0 copy-start.6
  0.7 2.4 %fusion.9 = (f32[1,1,1,1,2,256,256]{6,5,4,3,2,1,0:T(8,128)S(1)}, f32[1,1,1,1,2,256,256]{6,5,4,3,2,1,0:T(8,128)S(1)}, f32[1,1,1,1,2,256,256]{6,5,4,3,2,1,0:T(8,12...) fusion(f32[1,1,1,3,4,256,256]{6,5,4,3,2,1,0:T(8,128)} %param.9), kind=kLoop, calls=%fused_computation.22 | loop fusion | bytes 6291456 | tf_op jit(solution)/shard_map/slice | solution.py:187
  3.1 0.4 copy-done
  3.5 0.1 fusion
  4.3 0.0 copy-done.6
  4.3 0.6 fusion.8
  5.0 0.7 pad.10.clone
  5.7 0.1 pad.11.clone
  5.7 0.0 copy-start.4
  5.8 0.2 bitcast_select_fusion
  6.0 0.2 maximum_maximum_fusion.2
  6.2 1.3 %collective-permute-start.2 = (f32[520,256]{1,0:T(8,128)S(1)}, f32[520,256]{1,0:T(8,128)S(1)}, u32[]{:S(2)}, u32[]{:S(2)}) collective-permute-start(f32[520,256]{1,0:T(8,128)S(1)} %get-tuple-element.22), channel_id=1, source_target_pairs={{1,0},{2,1},{3,2},{4,3},{5,4},{6,5},{7,6},{9,8},{10,9},{11,10},{12... | collective-permute-start | bytes 1597448 | tf_op jit(solution)/shard_map/ppermute | solution.py:19
  7.5 9.4 %collective-permute-start = (f32[520,256]{1,0:T(8,128)S(1)}, f32[520,256]{1,0:T(8,128)S(1)}, u32[]{:S(2)}, u32[]{:S(2)}) collective-permute-start(f32[520,256]{1,0:T(8,128)S(1)} %get-tuple-element.24), channel_id=1, source_target_pairs={{32,0},{64,32},{96,64},{128,96},{160,128},{192,160},{224,192},{33,... | collective-permute-start | bytes 1597448 | tf_op jit(solution)/shard_map/ppermute | solution.py:19
  16.9 1.3 %collective-permute-start.1 = (f32[520,256]{1,0:T(8,128)S(1)}, f32[520,256]{1,0:T(8,128)S(1)}, u32[]{:S(2)}, u32[]{:S(2)}) collective-permute-start(f32[520,256]{1,0:T(8,128)S(1)} %get-tuple-element.23), channel_id=1, source_target_pairs={{8,0},{16,8},{24,16},{9,1},{17,9},{25,17},{10,2},{18,10},{26,18},{... | collective-permute-start | bytes 1597448 | tf_op jit(solution)/shard_map/ppermute | solution.py:19
  18.2 0.0 copy-done.4
  18.2 0.1 copy.12
  18.3 0.7 reshape_squeeze.3.picks_ref
  18.9 0.0 collective-permute-done.2.refs_0_
  18.9 0.0 copy-start.1
  18.9 0.8 copy-done.1
  19.7 26.3 %shard_map.95 = (f32[20,8,256]{2,1,0:T(8,128)}, f32[20,8,8]{2,1,0:T(8,128)}) custom-call(f32[1]{0:T(128)} %bitcast.1.scal_ref, s32[160]{0:T(256)} %reshape_squeeze.3.picks_ref, f32[3,4,256,256]{3,2,1,0:T(8,128)} %bitcast.43, f32[520,256]{1,0:T(8,128)} %copy-done.1, f32[2,8,256,256]{3,2,1,0:T(8,128)} %bitcast.45, f32[20,16,256]{2,1,0:T(8,128)} %bitcast.46), custom_call_target="tpu_custom_call" | custom-call | tf_op jit(solution)/shard_map/pallas_call | solution.py:146
  46.0 0.0 copy-start.5
  46.0 0.0 collective-permute-done.refs_0_
  46.0 0.0 copy-start.2
  46.1 7.4 %collective-permute-done.1.refs_1_ = f32[520,256]{1,0:T(8,128)S(1)} collective-permute-done((f32[520,256]{1,0:T(8,128)S(1)}, f32[520,256]{1,0:T(8,128)S(1)}, u32[]{:S(2)}, u32[]{:S(2)}) %collective-permute-start.1) | collective-permute-done | bytes 532512 | tf_op jit(solution)/shard_map/ppermute | solution.py:19
  53.5 0.0 copy-start.3
  53.5 0.0 copy-done.2
  53.5 0.8 copy-done.3
  54.3 19.1 %shard_map.96 = (f32[20,8,256]{2,1,0:T(8,128)}, f32[20,8,8]{2,1,0:T(8,128)}) custom-call(f32[1]{0:T(128)} %bitcast.1.scal_ref, s32[160]{0:T(256)} %reshape_squeeze.3.picks_ref, f32[3,4,256,256]{3,2,1,0:T(8,128)} %bitcast.44, f32[520,256]{1,0:T(8,128)} %copy-done.2, f32[520,256]{1,0:T(8,128)} %copy-done.3, ...), custom_call_target="tpu_custom_call", output_to_operand_aliasing={{0}: (6, {}), {1}: (7, {})} | custom-call | tf_op jit(solution)/shard_map/pallas_call | solution.py:146
  73.4 1.0 %copy.13 = f32[20,8,8]{0,2,1:T(8,128)S(1)} copy(f32[20,8,8]{2,1,0:T(8,128)} %get-tuple-element.9) | data formatting | bytes 10240 | tf_op jit(solution)/shard_map/pallas_call | solution.py:146
  74.4 0.0 copy-done.5
  74.4 0.2 fusion.3
  74.7 0.1 reshape.62
  74.8 10.0 %all_to_all.5 = f32[8,1,1024]{2,1,0:T(1,128)S(1)} all-to-all(f32[8,1,1024]{2,1,0:T(1,128)S(1)} %reshape.62), channel_id=1, replica_groups=mesh['gx'=8,'gy'=4,'gz'=8] {'gz'}, dimensions={0} | all-to-all | bytes 65536 | tf_op jit(solution)/shard_map/all_to_all | solution.py:210
  84.8 0.5 broadcast.35
  85.3 0.7 reduce
  86.1 0.1 reshape.63
  86.1 0.6 reduce_sum.49
  (4 shorter events, 0.1 us)
Async XLA Ops:
  0.7 2.8 %copy-start = (f32[1,1,1,3,4,256,256]{6,5,4,3,2,1,0:T(8,128)S(1)}, f32[1,1,1,3,4,256,256]{6,5,4,3,2,1,0:T(8,128)}, u32[]{:S(2)}) copy-start(f32[1,1,1,3,4,256,256]{6,5,4,3,2,1,0:T(8,128)} %param.9) | copy-start | bytes 9437188
  0.7 3.6 %copy-start.6 = (f32[4]{0:T(128)S(1)}, f32[4]{0:T(128)}, u32[]{:S(2)}) copy-start(f32[4]{0:T(128)} %param.15) | copy-start | bytes 52
  5.7 12.4 %copy-start.4 = (s32[1,1,1,20,8]{3,4,2,1,0:T(8,128)S(1)}, s32[1,1,1,20,8]{3,4,2,1,0:T(8,128)}, u32[]{:S(2)}) copy-start(s32[1,1,1,20,8]{3,4,2,1,0:T(8,128)} %param.12) | copy-start | bytes 1924
  6.2 12.7 %collective-permute-start.2 = (f32[520,256]{1,0:T(8,128)S(1)}, f32[520,256]{1,0:T(8,128)S(1)}, u32[]{:S(2)}, u32[]{:S(2)}) collective-permute-start(f32[520,256]{1,0:T(8,128)S(1)} %get-tuple-element.22), channel_id=1, source_target_pairs={{1,0},{2,1},{3,2},{4,3},{5,4},{6,5},{7,6},{9,8},{10,9},{11,10},{12... | collective-permute-start | bytes 1597448 | tf_op jit(solution)/shard_map/ppermute | solution.py:19
  7.5 38.5 %collective-permute-start = (f32[520,256]{1,0:T(8,128)S(1)}, f32[520,256]{1,0:T(8,128)S(1)}, u32[]{:S(2)}, u32[]{:S(2)}) collective-permute-start(f32[520,256]{1,0:T(8,128)S(1)} %get-tuple-element.24), channel_id=1, source_target_pairs={{32,0},{64,32},{96,64},{128,96},{160,128},{192,160},{224,192},{33,... | collective-permute-start | bytes 1597448 | tf_op jit(solution)/shard_map/ppermute | solution.py:19
  16.9 36.6 %collective-permute-start.1 = (f32[520,256]{1,0:T(8,128)S(1)}, f32[520,256]{1,0:T(8,128)S(1)}, u32[]{:S(2)}, u32[]{:S(2)}) collective-permute-start(f32[520,256]{1,0:T(8,128)S(1)} %get-tuple-element.23), channel_id=1, source_target_pairs={{8,0},{16,8},{24,16},{9,1},{17,9},{25,17},{10,2},{18,10},{26,18},{... | collective-permute-start | bytes 1597448 | tf_op jit(solution)/shard_map/ppermute | solution.py:19
  18.9 0.8 copy-start.1
  46.0 28.4 %copy-start.5 = (s32[1,1,1,20]{3,2,1,0:T(1,128)S(1)}, s32[1,1,1,20]{3,2,1,0:T(1,128)}, u32[]{:S(2)}) copy-start(s32[1,1,1,20]{3,2,1,0:T(1,128)} %param.13) | copy-start | bytes 244
  46.0 7.5 %copy-start.2 = (f32[520,256]{1,0:T(8,128)}, f32[520,256]{1,0:T(8,128)S(1)}, u32[]{:S(2)}) copy-start(f32[520,256]{1,0:T(8,128)S(1)} %collective-permute-done.refs_0_) | copy-start | bytes 1597444
  53.5 0.8 copy-start.3
